TPU v7x, 256 devices: a whole 4x4x8 slice. The times are simulated.
256 devices in a mesh: dp: 8 (over y, x_hi), shard: 32 (over x_lo, z, core).
Axes of the slice: x: 4 (x_hi: 2, x_lo: 2; x = x_hi * 2 + x_lo), y: 4, z: 8, core: 2. Of those that a mesh axis runs over, the one named last changes fastest.
Arguments:
- grads: float32 [8, 1, 2, 4096, 4096], P('dp', None, None, None, 'shard'), may hold values from -6 to 6
- params: float32 [1, 2, 4096, 4096], P(None, None, ('dp', 'shard')), may hold values from -0.09375 to 0.09375
- moment_one: float32 [1, 2, 4096, 4096], P(None, None, ('dp', 'shard')), may hold values from -0.75 to 0.75
- moment_two: float32 [1, 2, 4096, 4096], P(None, None, ('dp', 'shard')), may hold values from 1e-05 to 0.01
- relation_ids: int32 [1], replicated, may hold values from 0 to 63
- rates: float32 [64], replicated, may hold values from 0.02 to 0.1
- step_count: int32 [1], replicated, may hold values from 1 to 8
Outputs:
- new_params: float32 [1, 2, 4096, 4096], P(None, None, ('dp', 'shard'))
- new_moment_one: float32 [1, 2, 4096, 4096], P(None, None, ('dp', 'shard'))
- new_moment_two: float32 [1, 2, 4096, 4096], P(None, None, ('dp', 'shard'))
- panels: bfloat16 [1, 2, 4096, 4096], P(None, None, None, 'shard')
Inputs may be any that keep to these rules, and one draw needn't show every extreme that they name: `relation_ids`: relation ids are edge types. `step_count`: the step count is positive.
All inputs are finite; a program needn't handle non-finite values.
Results may differ from a plain program's by a relative error of at most 0.001.
Values may be sent and summed in bfloat16 or wider, within the bound.
No kernel may reach another device: no remote copies, remote signals or barrier semaphores. Data moves between devices by JAX's collectives and lax.ppermute only.
A program may use at most 128 MiB of HBM per device.

v0:
```python
import jax
import jax.numpy as jnp
from jax import lax
from jax.sharding import PartitionSpec as P


def body(grads, params, moment_one, moment_two, relation_ids, rates, step_count):
    groups = lax.axis_size("dp")
    owners = lax.axis_size("shard")
    relations = grads.shape[1]
    panel_cols = grads.shape[-1]
    width = panel_cols * owners
    owned = params.shape[2]
    pieces = grads.reshape(relations, 2, groups, owners, owned, panel_cols)
    moved = lax.all_to_all(pieces, "shard", split_axis=3, concat_axis=5, tiled=True)
    summed = lax.psum_scatter(moved, "dp", scatter_dimension=2, tiled=True)
    gradient = summed.reshape(relations, 2, owned, width) / groups
    onehot = (relation_ids[:, None] == jnp.arange(rates.shape[0], dtype=jnp.int32)[None, :]).astype(
        jnp.float32
    )
    learn = jnp.sum(onehot * rates[None, :], axis=1)[:, None, None, None]
    new_one = 0.9 * moment_one + 0.1 * gradient
    new_two = 0.95 * moment_two + 0.05 * gradient * gradient
    steps = step_count[0].astype(jnp.float32)
    fix_one = 1.0 - jnp.power(jnp.float32(0.9), steps)
    fix_two = 1.0 - jnp.power(jnp.float32(0.95), steps)
    update = new_one / fix_one / (jnp.sqrt(new_two / fix_two) + 1e-08) + 0.1 * params
    new_params = params - learn * update
    fresh = new_params.astype(jnp.bfloat16).reshape(relations, 2, 1, 1, owned, width)
    stacked = lax.all_gather(fresh, "dp", axis=2, tiled=True)
    panel = lax.all_to_all(stacked, "shard", split_axis=5, concat_axis=3, tiled=True)
    panels = panel.reshape(relations, 2, width, panel_cols)
    return (new_params, new_one, new_two, panels)


def solution(mesh):
    in_specs = (
        P("dp", None, None, None, "shard"),
        P(None, None, ("dp", "shard"), None),
        P(None, None, ("dp", "shard"), None),
        P(None, None, ("dp", "shard"), None),
        P(),
        P(),
        P(),
    )
    out_specs = (
        P(None, None, ("dp", "shard"), None),
        P(None, None, ("dp", "shard"), None),
        P(None, None, ("dp", "shard"), None),
        P(None, None, None, "shard"),
    )
    return jax.shard_map(body, mesh=mesh, in_specs=in_specs, out_specs=out_specs, check_vma=False)
```

profile of v0, /device:TPU:32, one launch (start us, length us, event | category | flops | bytes accessed | tf_op | source)
XLA Modules:
  0.0 405.4 jit_solution(11220922597998962744)
XLA Ops:
  7.2 0.0 reduce-scatter.2.cloned.1.call-start
  7.2 2.8 copy.31
  10.1 105.8 %all_to_all.33 = f32[1,2,8,32,16,128]{5,4,1,2,0,3:T(8,128)S(1)} all-to-all(f32[1,2,8,32,16,128]{5,4,1,2,0,3:T(8,128)S(1)} %copy.31), channel_id=1, replica_groups=mesh['dp'=8,'shard'=32] {'shard'}, dimensions={3} | all-to-all | bytes 8388608 | tf_op jit(solution)/shard_map/all_to_all | solution.py:15
  115.9 2.4 copy.32
  118.3 5.7 %copy.33 = f32[1,2,8,1,16,4096]{5,4,3,1,0,2:T(8,128)} copy(f32[1,2,8,1,16,4096]{5,3,4,2,1,0:T(1,128)S(1)} %bitcast.38) | data formatting | bytes 8388608 | tf_op jit(solution)/shard_map/all_to_all | solution.py:15
  124.0 0.0 copy-start.3
  124.0 0.0 copy-start
  124.1 0.0 reduce-scatter.2.cloned.1.call-update
  124.1 0.0 all-gather.3.cloned.1.call-start
  125.6 0.0 copy-done.3
  125.6 0.7 fusion.1
  126.3 85.0 %reduce-scatter.2.cloned.1.call-done = f32[1,2,1,1,16,4096]{5,4,3,1,0,2:T(8,128)} async-done(((f32[1,2,8,1,16,4096]{5,4,3,1,0,2:T(8,128)}), f32[1,2,1,1,16,4096]{5,4,3,1,0,2:T(8,128)}) %reduce-scatter.2.cloned.1.call-update) | async-done | bytes 524304 | tf_op jit(solution)/shard_map/reduce_scatter | solution.py:16
  211.3 0.0 copy-done
  211.3 0.0 copy-done.1
  211.3 0.0 copy-done.2
  211.3 3.2 fusion.2
  214.5 0.0 all-gather.3.cloned.1.call-update
  214.6 57.6 %all-gather.3.cloned.1.call-done = bf16[1,2,128,4096]{3,2,1,0:T(8,128)(2,1)} async-done(((bf16[1,2,16,4096]{3,2,1,0:T(8,128)(2,1)}), bf16[1,2,128,4096]{3,2,1,0:T(8,128)(2,1)}) %all-gather.3.cloned.1.call-update) | async-done | bytes 2097168 | tf_op jit(solution)/shard_map/all_gather | solution.py:30
  272.1 15.3 %copy.37 = bf16[1,2,8,1,16,4096]{4,2,1,3,0,5:T(8,128)(2,1)} copy(bf16[1,2,8,1,16,4096]{5,4,2,1,3,0:T(8,128)(2,1)} %bitcast.41) | data formatting | bytes 4194304 | tf_op jit(solution)/shard_map/all_gather | solution.py:30
  287.4 19.7 %reshape.90 = bf16[32,2,16384]{2,1,0:T(2,128)(2,1)S(1)} reshape(bf16[4096,1,1,2,8,16]{5,4,3,2,1,0:T(8,128)(2,1)} %bitcast.36) | data formatting | bytes 4194304
  307.2 59.0 %all_to_all.34 = bf16[32,2,16384]{2,1,0:T(2,128)(2,1)} all-to-all(bf16[32,2,16384]{2,1,0:T(2,128)(2,1)S(1)} %reshape.90), channel_id=1, replica_groups=mesh['dp'=8,'shard'=32] {'shard'}, dimensions={0} | all-to-all | bytes 4194304 | tf_op jit(solution)/shard_map/all_to_all | solution.py:31
  366.2 16.4 %reshape.91 = bf16[4096,1,1,2,8,16]{5,4,3,2,1,0:T(8,128)(2,1)} reshape(bf16[32,2,16384]{2,1,0:T(2,128)(2,1)} %all_to_all.34) | data formatting | bytes 4194304
  382.6 13.7 %copy.40 = bf16[1,2,8,1,16,32,128]{6,5,4,2,1,3,0:T(8,128)(2,1)S(1)} copy(bf16[1,2,8,1,16,32,128]{4,2,1,6,5,3,0:T(8,128)(2,1)} %bitcast.37) | data formatting | bytes 4194304 | tf_op jit(solution)/shard_map/all_to_all | solution.py:31
  396.4 2.2 copy.39
  (2 shorter events, 0.0 us)
Async XLA Ops:
  7.2 204.2 %reduce-scatter.2.cloned.1.call-start = ((), (), s32[]{:S(2)}) async-start(), calls=%async_computation.3 | async-start | bytes 4718592 | tf_op jit(solution)/shard_map/reduce_scatter | solution.py:16
  124.0 1.6 copy-start.3
  124.0 87.3 %copy-start = (f32[1,2,16,4096]{3,2,1,0:T(8,128)S(1)}, f32[1,2,16,4096]{3,2,1,0:T(8,128)}, u32[]{:S(2)}) copy-start(f32[1,2,16,4096]{3,2,1,0:T(8,128)} %param.8) | copy-start | bytes 1572868
  124.0 87.3 %copy-start.1 = (f32[1,2,16,4096]{3,2,1,0:T(8,128)S(1)}, f32[1,2,16,4096]{3,2,1,0:T(8,128)}, u32[]{:S(2)}) copy-start(f32[1,2,16,4096]{3,2,1,0:T(8,128)} %param.10) | copy-start | bytes 1572868
  124.0 87.3 %copy-start.2 = (f32[1,2,16,4096]{3,2,1,0:T(8,128)S(1)}, f32[1,2,16,4096]{3,2,1,0:T(8,128)}, u32[]{:S(2)}) copy-start(f32[1,2,16,4096]{3,2,1,0:T(8,128)} %param.9) | copy-start | bytes 1572868
  124.1 148.1 %all-gather.3.cloned.1.call-start = ((), (), s32[]{:S(2)}) async-start(), calls=%async_computation.4 | async-start | bytes 2359296 | tf_op jit(solution)/shard_map/all_gather | solution.py:30
Sparse Core Ops, SparseCore 0:
  124.2 87.0 reduce-scatter.1
  214.7 57.4 all-gather.2
where the time goes:
time: 407 us; the launch traced here: 405 us
  blocking collectives  165 us (41%)
  waiting for transfers between devices  143 us (35%)
  local copies, waits for them, and re-layouts  78.4 us (19%)
  between operations  15.6 us (4%)
    all_to_all x1, blocking collectives, body(): lax.all_to_all(pieces, 'shard', split_axis=3, concat_axis=5, tiled=True)  106 us
    reduce_scatter x1, waiting for transfers between devices, body(): summed = lax.psum_scatter(moved, 'dp', scatter_dimension=2, tiled=True)  85 us
    all_to_all x1, blocking collectives, body(): lax.all_to_all(stacked, 'shard', split_axis=5, concat_axis=3, tiled=True)  59 us
    all_gather x1, waiting for transfers between devices, body(): stacked = lax.all_gather(fresh, 'dp', axis=2, tiled=True)  57.6 us
    unnamed x10, local copies, waits for them, and re-layouts  36.2 us
    all_to_all x2, local copies, waits for them, and re-layouts, body(): lax.all_to_all(stacked, 'shard', split_axis=5, concat_axis=3, tiled=True)  15.9 us
    all_gather x1, local copies, waits for them, and re-layouts, body(): stacked = lax.all_gather(fresh, 'dp', axis=2, tiled=True)  15.3 us
    all_to_all x2, local copies, waits for them, and re-layouts, body(): lax.all_to_all(pieces, 'shard', split_axis=3, concat_axis=5, tiled=True)  8.15 us
  transfers between devices with their start and end apart: 2, of which 2 were waited for; matrix products, arithmetic and copies ran while one was open for 0% of the time, Pallas kernels for 0%

commit v1 on v0

--- a/solution.py
+++ b/solution.py
@@ -8,13 +8,15 @@
     groups = lax.axis_size("dp")
     owners = lax.axis_size("shard")
     relations = grads.shape[1]
+    rows = grads.shape[3]
     panel_cols = grads.shape[-1]
     width = panel_cols * owners
     owned = params.shape[2]
-    pieces = grads.reshape(relations, 2, groups, owners, owned, panel_cols)
-    moved = lax.all_to_all(pieces, "shard", split_axis=3, concat_axis=5, tiled=True)
-    summed = lax.psum_scatter(moved, "dp", scatter_dimension=2, tiled=True)
-    gradient = summed.reshape(relations, 2, owned, width) / groups
+    block = rows // groups
+    summed = lax.psum_scatter(grads[0], "dp", scatter_dimension=2, tiled=True)
+    pieces = summed.reshape(relations, 2, owners, owned, panel_cols)
+    moved = lax.all_to_all(pieces, "shard", split_axis=2, concat_axis=2, tiled=True)
+    gradient = moved.transpose(0, 1, 3, 2, 4).reshape(relations, 2, owned, width) / groups
     onehot = (relation_ids[:, None] == jnp.arange(rates.shape[0], dtype=jnp.int32)[None, :]).astype(
         jnp.float32
     )
@@ -26,10 +28,11 @@
     fix_two = 1.0 - jnp.power(jnp.float32(0.95), steps)
     update = new_one / fix_one / (jnp.sqrt(new_two / fix_two) + 1e-08) + 0.1 * params
     new_params = params - learn * update
-    fresh = new_params.astype(jnp.bfloat16).reshape(relations, 2, 1, 1, owned, width)
-    stacked = lax.all_gather(fresh, "dp", axis=2, tiled=True)
-    panel = lax.all_to_all(stacked, "shard", split_axis=5, concat_axis=3, tiled=True)
-    panels = panel.reshape(relations, 2, width, panel_cols)
+    fresh = new_params.astype(jnp.bfloat16).reshape(relations, 2, owned, owners, panel_cols)
+    fresh = fresh.transpose(0, 1, 3, 2, 4)
+    back = lax.all_to_all(fresh, "shard", split_axis=2, concat_axis=2, tiled=True)
+    back = back.reshape(relations, 2, block, panel_cols)
+    panels = lax.all_gather(back, "dp", axis=2, tiled=True)
     return (new_params, new_one, new_two, panels)
 
 

time: 407 us -> 217 us (0.53)
  blocking collectives: 165 us -> 15.8 us
  local copies, waits for them, and re-layouts: 78.4 us -> 5.83 us
  waiting for transfers between devices: 143 us -> 167 us
  starting transfers between devices: 0.08 us -> 7.72 us
    all_to_all x2 -> x1, blocking collectives: 165 us -> 15.8 us  [body(): lax.all_to_all(fresh, 'shard', split_axis=2, concat_axis=2, tiled=True)]
    unnamed x10, local copies, waits for them, and re-layouts: 36.2 us -> 3.1 us
    all_to_all x4 -> x1, local copies, waits for them, and re-layouts: 24.1 us -> 0.72 us  [body(): lax.all_to_all(fresh, 'shard', split_axis=2, concat_axis=2, tiled=True)]
    all_to_all x0 -> x1, waiting for transfers between devices: none -> 15.6 us  [body(): lax.all_to_all(pieces, 'shard', split_axis=2, concat_axis=2, tiled=True)]
    all_gather x1 -> x0, local copies, waits for them, and re-layouts: 15.3 us -> none  [body(): stacked = lax.all_gather(fresh, 'dp', axis=2, tiled=True)]
    reduce_scatter x1, waiting for transfers between devices: 85 us -> 96.8 us  [body(): summed = lax.psum_scatter(grads[0], 'dp', scatter_dimension=2, tiled=True)]
    all_to_all x0 -> x1, starting transfers between devices: none -> 7.64 us  [body(): lax.all_to_all(pieces, 'shard', split_axis=2, concat_axis=2, tiled=True)]
  transfers between devices with their start and end apart: 2 -> 3, of which waited for: 2 -> 3; matrix products, arithmetic and copies ran while one was open for 0% -> 0% of each run, Pallas kernels for 0% -> 0%
where the time goes in v1:
time: 217 us; the launch traced here: 216 us
  waiting for transfers between devices  167 us (77%)
  blocking collectives  15.8 us (7%)
  between operations  15.5 us (7%)
  starting transfers between devices  7.72 us (4%)
  local copies, waits for them, and re-layouts  5.83 us (3%)
  other arithmetic  3.57 us (2%)
    reduce_scatter x1, waiting for transfers between devices, body(): summed = lax.psum_scatter(grads[0], 'dp', scatter_dimension=2, tiled=True)  96.8 us
    all_gather x1, waiting for transfers between devices, body(): panels = lax.all_gather(back, 'dp', axis=2, tiled=True)  54.3 us
    all_to_all x1, blocking collectives, body(): lax.all_to_all(fresh, 'shard', split_axis=2, concat_axis=2, tiled=True)  15.8 us
    all_to_all x1, waiting for transfers between devices, body(): lax.all_to_all(pieces, 'shard', split_axis=2, concat_axis=2, tiled=True)  15.6 us
    all_to_all x1, starting transfers between devices, body(): lax.all_to_all(pieces, 'shard', split_axis=2, concat_axis=2, tiled=True)  7.64 us
  transfers between devices with their start and end apart: 3, of which 3 were waited for; matrix products, arithmetic and copies ran while one was open for 0% of the time, Pallas kernels for 0%

profile of v1, /device:TPU:32, one launch (start us, length us, event | category | flops | bytes accessed | tf_op | source)
XLA Modules:
  0.0 215.9 jit_solution(13947312932788557129)
XLA Ops:
  7.2 0.0 reduce-scatter.2.cloned.1.call-start
  7.2 0.7 reduce-scatter.2.cloned.1.call-update
  7.9 0.0 copy-start.3
  7.9 0.0 copy-start
  7.9 0.0 copy-start.1
  7.9 0.0 copy-start.2
  7.9 96.8 %reduce-scatter.2.cloned.1.call-done = f32[1,2,512,128]{3,2,1,0:T(8,128)} async-done(((f32[1,2,4096,128]{3,2,1,0:T(8,128)}), f32[1,2,512,128]{3,2,1,0:T(8,128)}) %reduce-scatter.2.cloned.1.call-update) | async-done | bytes 524304 | tf_op jit(solution)/shard_map/reduce_scatter | solution.py:16
  104.7 1.9 copy.29
  106.6 7.6 %all-to-all-start = ((f32[1,2,32,16,128]{4,3,1,0,2:T(8,128)}), f32[1,2,32,16,128]{4,3,1,0,2:T(8,128)S(1)}, u32[]{:S(2)}, u32[]{:S(2)}) async-start(f32[1,2,32,16,128]{4,3,1,0,2:T(8,128)} %copy.29), calls=%async_computation.1 | async-start | bytes 1048576 | tf_op jit(solution)/shard_map/all_to_all | solution.py:18
  114.3 0.0 all-gather.2.cloned.1.call-start
  115.7 0.0 copy-done.3
  115.7 0.7 fusion
  116.4 15.6 %all-to-all-done = f32[1,2,32,16,128]{4,3,1,0,2:T(8,128)S(1)} async-done(((f32[1,2,32,16,128]{4,3,1,0,2:T(8,128)}), f32[1,2,32,16,128]{4,3,1,0,2:T(8,128)S(1)}, u32[]{:S(2)}, u32[]{:S(2)}) %all-to-all-start) | async-done | bytes 524320 | tf_op jit(solution)/shard_map/all_to_all | solution.py:18
  132.0 0.4 copy_multiply_fusion
  132.4 0.0 copy-done
  132.4 0.0 copy-done.1
  132.4 0.0 copy-done.2
  132.4 2.5 %fusion.1 = (bf16[1,2,16,4096]{3,2,1,0:T(8,128)(2,1)S(1)}, f32[1,2,16,4096]{3,2,1,0:T(8,128)}, f32[1,2,16,4096]{3,2,1,0:T(8,128)}, f32[1,2,16,4096]{3,2,1,0:T(8,128)}) fusion(f32[1,2,16,4096]{3,2,1,0:T(8,128)S(1)} %copy-done, f32[]{:T(128)} %bitcast.8, f32[]{:T(128)} %bitcast.5, f32[]{:T(128)} %fusion, f32[1,2,16,4096]{3,0,2,1:T(1,128)S(1)} %bitcast.22, ...), kind=kLoop, calls=%fused_computation.7 | loop fusion | flops 1703936 | bytes 4456460 | tf_op jit(solution)/shard_map/convert_element_type | solution.py:31
  135.0 0.1 copy.35
  135.1 15.8 %all_to_all.10 = bf16[1,2,32,16,128]{4,3,1,0,2:T(8,128)(2,1)S(1)} all-to-all(bf16[1,2,32,16,128]{4,3,1,0,2:T(8,128)(2,1)S(1)} %copy.35), channel_id=1, replica_groups=mesh['dp'=8,'shard'=32] {'shard'}, dimensions={2} | all-to-all | bytes 524288 | tf_op jit(solution)/shard_map/all_to_all | solution.py:33
  150.9 0.7 copy.36
  151.6 0.0 all-gather.2.cloned.1.call-update
  151.7 54.3 %all-gather.2.cloned.1.call-done = bf16[1,2,4096,128]{3,2,1,0:T(8,128)(2,1)} async-done(((bf16[1,2,512,128]{3,2,1,0:T(8,128)(2,1)}), bf16[1,2,4096,128]{3,2,1,0:T(8,128)(2,1)}) %all-gather.2.cloned.1.call-update) | async-done | bytes 2097168 | tf_op jit(solution)/shard_map/all_gather | solution.py:35
  206.0 3.0 %copy.47 = bf16[1,2,4096,128]{3,2,1,0:T(8,128)(2,1)} copy(bf16[1,2,4096,128]{3,2,1,0:T(8,128)(2,1)} %all-gather.2.cloned.1.call-done) | data formatting | bytes 4194304
  (1 shorter events, 0.0 us)
Async XLA Ops:
  7.2 97.6 %reduce-scatter.2.cloned.1.call-start = ((), (), s32[]{:S(2)}) async-start(), calls=%async_computation.3 | async-start | bytes 4718592 | tf_op jit(solution)/shard_map/reduce_scatter | solution.py:16
  7.9 107.8 %copy-start.3 = (f32[64]{0:T(128)S(1)}, f32[64]{0:T(128)}, u32[]{:S(2)}) copy-start(f32[64]{0:T(128)} %param.12) | copy-start | bytes 772
  7.9 124.5 %copy-start = (f32[1,2,16,4096]{3,2,1,0:T(8,128)S(1)}, f32[1,2,16,4096]{3,2,1,0:T(8,128)}, u32[]{:S(2)}) copy-start(f32[1,2,16,4096]{3,2,1,0:T(8,128)} %param.8) | copy-start | bytes 1572868
  7.9 124.5 %copy-start.1 = (f32[1,2,16,4096]{3,2,1,0:T(8,128)S(1)}, f32[1,2,16,4096]{3,2,1,0:T(8,128)}, u32[]{:S(2)}) copy-start(f32[1,2,16,4096]{3,2,1,0:T(8,128)} %param.10) | copy-start | bytes 1572868
  7.9 124.5 %copy-start.2 = (f32[1,2,16,4096]{3,2,1,0:T(8,128)S(1)}, f32[1,2,16,4096]{3,2,1,0:T(8,128)}, u32[]{:S(2)}) copy-start(f32[1,2,16,4096]{3,2,1,0:T(8,128)} %param.9) | copy-start | bytes 1572868
  106.6 25.4 %all-to-all-start = ((f32[1,2,32,16,128]{4,3,1,0,2:T(8,128)}), f32[1,2,32,16,128]{4,3,1,0,2:T(8,128)S(1)}, u32[]{:S(2)}, u32[]{:S(2)}) async-start(f32[1,2,32,16,128]{4,3,1,0,2:T(8,128)} %copy.29), calls=%async_computation.1 | async-start | bytes 1048576 | tf_op jit(solution)/shard_map/all_to_all | solution.py:18
  114.3 91.7 %all-gather.2.cloned.1.call-start = ((), (), s32[]{:S(2)}) async-start(), calls=%async_computation.4 | async-start | bytes 2359296 | tf_op jit(solution)/shard_map/all_gather | solution.py:35
Sparse Core Ops, SparseCore 0:
  12.1 92.6 reduce-scatter.1
  151.8 54.1 all-gather.1

commit v2 on v1

--- a/solution.py
+++ b/solution.py
@@ -2,6 +2,55 @@
 import jax.numpy as jnp
 from jax import lax
 from jax.sharding import PartitionSpec as P
+
+
+def _dp_rings(groups):
+    ring = groups // 2
+    plus = [(2 * y + h, 2 * ((y + 1) % ring) + h) for y in range(ring) for h in range(2)]
+    minus = [(2 * y + h, 2 * ((y - 1) % ring) + h) for y in range(ring) for h in range(2)]
+    partner = [(2 * y + h, 2 * y + 1 - h) for y in range(ring) for h in range(2)]
+    return ring, plus, minus, partner
+
+
+def _take(x, index):
+    return lax.dynamic_index_in_dim(x, index, axis=1, keepdims=False)
+
+
+def _reduce_scatter_dp(x, groups):
+    ring, plus, minus, partner = _dp_rings(groups)
+    d = lax.axis_index("dp")
+    y = d // 2
+    h = d % 2
+    even = x[:, :, 0]
+    odd = x[:, :, 1]
+    up = _take(even, (y - 1) % ring)
+    down = _take(odd, (y + 1) % ring)
+    for t in range(ring - 1):
+        up = lax.ppermute(up, "dp", plus) + _take(even, (y - t - 2) % ring)
+        down = lax.ppermute(down, "dp", minus) + _take(odd, (y + t + 2) % ring)
+    keep = lax.select(h == 0, up, down)
+    send = lax.select(h == 0, down, up)
+    return keep + lax.ppermute(send, "dp", partner)
+
+
+def _all_gather_dp(mine, groups):
+    ring, plus, minus, partner = _dp_rings(groups)
+    d = lax.axis_index("dp")
+    y = d // 2
+    h = d % 2
+    other = lax.ppermute(mine, "dp", partner)
+    even = lax.select(h == 0, mine, other)
+    odd = lax.select(h == 0, other, mine)
+    lead, block, cols = mine.shape
+    out = jnp.zeros((lead, ring, 2, block, cols), mine.dtype)
+    out = lax.dynamic_update_slice(out, jnp.stack([even, odd], axis=1)[:, None], (0, y, 0, 0, 0))
+    up, down = even, odd
+    for t in range(ring - 1):
+        up = lax.ppermute(up, "dp", plus)
+        down = lax.ppermute(down, "dp", minus)
+        out = lax.dynamic_update_slice(out, up[:, None, None], (0, (y - t - 1) % ring, 0, 0, 0))
+        out = lax.dynamic_update_slice(out, down[:, None, None], (0, (y + t + 1) % ring, 1, 0, 0))
+    return out.reshape(lead, groups * block, cols)
 
 
 def body(grads, params, moment_one, moment_two, relation_ids, rates, step_count):
@@ -13,7 +62,9 @@
     width = panel_cols * owners
     owned = params.shape[2]
     block = rows // groups
-    summed = lax.psum_scatter(grads[0], "dp", scatter_dimension=2, tiled=True)
+    lead = relations * 2
+    local = grads.reshape(lead, groups // 2, 2, block, panel_cols)
+    summed = _reduce_scatter_dp(local, groups)
     pieces = summed.reshape(relations, 2, owners, owned, panel_cols)
     moved = lax.all_to_all(pieces, "shard", split_axis=2, concat_axis=2, tiled=True)
     gradient = moved.transpose(0, 1, 3, 2, 4).reshape(relations, 2, owned, width) / groups
@@ -31,8 +82,8 @@
     fresh = new_params.astype(jnp.bfloat16).reshape(relations, 2, owned, owners, panel_cols)
     fresh = fresh.transpose(0, 1, 3, 2, 4)
     back = lax.all_to_all(fresh, "shard", split_axis=2, concat_axis=2, tiled=True)
-    back = back.reshape(relations, 2, block, panel_cols)
-    panels = lax.all_gather(back, "dp", axis=2, tiled=True)
+    back = back.reshape(lead, block, panel_cols)
+    panels = _all_gather_dp(back, groups).reshape(relations, 2, rows, panel_cols)
     return (new_params, new_one, new_two, panels)
 
 

time: 217 us -> 153 us (0.71)
  waiting for transfers between devices: 167 us -> 76.2 us
  starting transfers between devices: 7.72 us -> 36 us
  between operations: 15.5 us -> 2.26 us
  other arithmetic: 3.57 us -> 11.4 us
  local copies, waits for them, and re-layouts: 5.83 us -> 9.77 us
    reduce_scatter x1 -> x0, waiting for transfers between devices: 96.8 us -> none  [body(): summed = lax.psum_scatter(grads[0], 'dp', scatter_dimension=2, tiled=True)]
    ppermute x0 -> x14, waiting for transfers between devices: none -> 60.5 us  [the longest x3 24 us: _reduce_scatter_dp(): down = lax.ppermute(down, 'dp', minus) + _take(odd, (y + t + 2) % ring)]
    all_gather x1 -> x0, waiting for transfers between devices: 54.3 us -> none  [body(): panels = lax.all_gather(back, 'dp', axis=2, tiled=True)]
    ppermute x0 -> x14, starting transfers between devices: none -> 26.3 us  [the longest x3 10.2 us: _reduce_scatter_dp(): down = lax.ppermute(down, 'dp', minus) + _take(odd, (y + t + 2) % ring)]
    add x0 -> x5, other arithmetic: none -> 6.63 us  [the longest x2 3.78 us: _reduce_scatter_dp(): up = lax.ppermute(up, 'dp', plus) + _take(even, (y - t - 2) % ring)]
    slice x0 -> x1, local copies, waits for them, and re-layouts: none -> 3.95 us  [_reduce_scatter_dp(): odd = x[:, :, 1]]
    squeeze x0 -> x2, local copies, waits for them, and re-layouts: none -> 2.7 us  [_take(): return lax.dynamic_index_in_dim(x, index, axis=1, keepdims=False)]
  transfers between devices with their start and end apart: 3 -> 15, of which waited for: 3 -> 12; matrix products, arithmetic and copies ran while one was open for 0% -> 6% of each run, Pallas kernels for 0% -> 0%
where the time goes in v2:
time: 153 us; the launch traced here: 151 us
  waiting for transfers between devices  76.2 us (50%)
  starting transfers between devices  36 us (24%)
  blocking collectives  15.8 us (10%)
  other arithmetic  11.4 us (7%)
  local copies, waits for them, and re-layouts  9.77 us (6%)
  between operations  2.26 us (1%)
    ppermute x3, waiting for transfers between devices, _reduce_scatter_dp(): down = lax.ppermute(down, 'dp', minus) + _take(odd, (y + t + 2) % ring)  24 us
    all_to_all x1, blocking collectives, body(): lax.all_to_all(fresh, 'shard', split_axis=2, concat_axis=2, tiled=True)  15.8 us
    all_to_all x1, waiting for transfers between devices, body(): lax.all_to_all(pieces, 'shard', split_axis=2, concat_axis=2, tiled=True)  15.7 us
    ppermute x3, waiting for transfers between devices, _all_gather_dp(): up = lax.ppermute(up, 'dp', plus)  12.3 us
    ppermute x3, starting transfers between devices, _reduce_scatter_dp(): down = lax.ppermute(down, 'dp', minus) + _take(odd, (y + t + 2) % ring)  10.2 us
    ppermute x3, starting transfers between devices, _all_gather_dp(): down = lax.ppermute(down, 'dp', minus)  10.1 us
    all_to_all x1, starting transfers between devices, body(): lax.all_to_all(pieces, 'shard', split_axis=2, concat_axis=2, tiled=True)  9.66 us
    ppermute x1, waiting for transfers between devices, _reduce_scatter_dp(): return keep + lax.ppermute(send, 'dp', partner)  9.3 us
  transfers between devices with their start and end apart: 15, of which 12 were waited for; matrix products, arithmetic and copies ran while one was open for 6% of the time, Pallas kernels for 0%

profile of v2, /device:TPU:32, one launch (start us, length us, event | category | flops | bytes accessed | tf_op | source)
XLA Modules:
  0.0 151.4 jit_solution(8406576736947991927)
XLA Ops:
  0.7 4.0 %fusion.3 = (f32[2,4,1,512,128]{4,3,2,1,0:T(8,128)S(1)}, f32[2,4,1,512,128]{4,3,2,1,0:T(8,128)}) fusion(f32[2,4,2,512,128]{4,3,2,1,0:T(8,128)} %bitcast.81), kind=kLoop, calls=%fused_computation.28 | loop fusion | bytes 8388608 | tf_op jit(solution)/shard_map/slice | solution.py:25
  5.4 3.0 %collective-permute-start.3 = (f32[2,512,128]{2,1,0:T(8,128)}, f32[2,512,128]{2,1,0:T(8,128)S(1)}, u32[]{:S(2)}, u32[]{:S(2)}) collective-permute-start(f32[2,512,128]{2,1,0:T(8,128)} %dynamic-slice_bitcast_fusion), channel_id=1, source_target_pairs={{0,192},{32,224},{64,0},{96,32},{128,64},{160,96},{192,128},{224,1... | collective-permute-start | bytes 1572872 | tf_op jit(solution)/shard_map/ppermute | solution.py:30
  10.3 9.6 %collective-permute-done.3 = f32[2,512,128]{2,1,0:T(8,128)S(1)} collective-permute-done((f32[2,512,128]{2,1,0:T(8,128)}, f32[2,512,128]{2,1,0:T(8,128)S(1)}, u32[]{:S(2)}, u32[]{:S(2)}) %collective-permute-start.3) | collective-permute-done | bytes 524320 | tf_op jit(solution)/shard_map/ppermute | solution.py:30
  20.8 3.6 %collective-permute-start.4 = (f32[2,512,128]{2,1,0:T(8,128)}, f32[2,512,128]{2,1,0:T(8,128)S(1)}, u32[]{:S(2)}, u32[]{:S(2)}) collective-permute-start(f32[2,512,128]{2,1,0:T(8,128)} %bitcast_add_fusion.2), channel_id=1, source_target_pairs={{0,192},{32,224},{64,0},{96,32},{128,64},{160,96},{192,128},{224,1... | collective-permute-start | bytes 1572872 | tf_op jit(solution)/shard_map/ppermute | solution.py:30
  25.1 1.9 %bitcast_add_fusion.5 = f32[2,512,128]{2,1,0:T(8,128)} fusion(f32[2,512,128]{2,1,0:T(8,128)S(1)} %collective-permute-done, f32[2,4,1,512,128]{4,3,2,1,0:T(8,128)} %get-tuple-element.13, s32[]{:T(128)S(6)} %select_n.116), kind=kLoop, calls=%fused_computation.7 | loop fusion | flops 131072 | bytes 1572868 | tf_op jit(solution)/shard_map/add | solution.py:29
  27.0 8.0 %collective-permute-done.4 = f32[2,512,128]{2,1,0:T(8,128)S(1)} collective-permute-done((f32[2,512,128]{2,1,0:T(8,128)}, f32[2,512,128]{2,1,0:T(8,128)S(1)}, u32[]{:S(2)}, u32[]{:S(2)}) %collective-permute-start.4) | collective-permute-done | bytes 524320 | tf_op jit(solution)/shard_map/ppermute | solution.py:30
  35.9 3.6 %collective-permute-start.5 = (f32[2,512,128]{2,1,0:T(8,128)}, f32[2,512,128]{2,1,0:T(8,128)S(1)}, u32[]{:S(2)}, u32[]{:S(2)}) collective-permute-start(f32[2,512,128]{2,1,0:T(8,128)} %bitcast_add_fusion.1), channel_id=1, source_target_pairs={{0,192},{32,224},{64,0},{96,32},{128,64},{160,96},{192,128},{224,1... | collective-permute-start | bytes 1572872 | tf_op jit(solution)/shard_map/ppermute | solution.py:30
  41.0 1.9 %bitcast_add_fusion.4 = f32[2,512,128]{2,1,0:T(8,128)} fusion(f32[2,512,128]{2,1,0:T(8,128)S(1)} %collective-permute-done.1, f32[2,4,1,512,128]{4,3,2,1,0:T(8,128)} %get-tuple-element.13, s32[]{:T(128)S(6)} %select_n.118), kind=kLoop, calls=%fused_computation.6 | loop fusion | flops 131072 | bytes 1572868 | tf_op jit(solution)/shard_map/add | solution.py:29
  42.9 6.4 %collective-permute-done.5 = f32[2,512,128]{2,1,0:T(8,128)S(1)} collective-permute-done((f32[2,512,128]{2,1,0:T(8,128)}, f32[2,512,128]{2,1,0:T(8,128)S(1)}, u32[]{:S(2)}, u32[]{:S(2)}) %collective-permute-start.5) | collective-permute-done | bytes 524320 | tf_op jit(solution)/shard_map/ppermute | solution.py:30
  49.3 6.7 %collective-permute-done.2 = f32[2,512,128]{2,1,0:T(8,128)S(1)} collective-permute-done((f32[2,512,128]{2,1,0:T(8,128)}, f32[2,512,128]{2,1,0:T(8,128)S(1)}, u32[]{:S(2)}, u32[]{:S(2)}) %collective-permute-start.2) | collective-permute-done | bytes 524320 | tf_op jit(solution)/shard_map/ppermute | solution.py:29
  57.1 3.1 %collective-permute-start.6 = (f32[2,512,128]{2,1,0:T(8,128)S(1)}, f32[2,512,128]{2,1,0:T(8,128)S(1)}, u32[]{:S(2)}, u32[]{:S(2)}) collective-permute-start(f32[2,512,128]{2,1,0:T(8,128)S(1)} %broadcast_select_fusion.2), channel_id=1, source_target_pairs={{0,32},{32,0},{64,96},{96,64},{128,160},{160,128},{192,224},{224,1... | collective-permute-start | bytes 1572872 | tf_op jit(solution)/shard_map/ppermute | solution.py:33
  60.2 9.3 %collective-permute-done.6 = f32[2,512,128]{2,1,0:T(8,128)S(1)} collective-permute-done((f32[2,512,128]{2,1,0:T(8,128)S(1)}, f32[2,512,128]{2,1,0:T(8,128)S(1)}, u32[]{:S(2)}, u32[]{:S(2)}) %collective-permute-start.6) | collective-permute-done | bytes 524320 | tf_op jit(solution)/shard_map/ppermute | solution.py:33
  71.6 9.7 %all-to-all-start = ((f32[1,2,32,16,128]{4,3,1,0,2:T(8,128)}), f32[1,2,32,16,128]{4,3,1,0,2:T(8,128)S(1)}, u32[]{:S(2)}, u32[]{:S(2)}) async-start(f32[1,2,32,16,128]{4,3,1,0,2:T(8,128)} %copy.47), calls=%async_computation | async-start | bytes 1048576 | tf_op jit(solution)/shard_map/all_to_all | solution.py:69
  83.3 15.7 %all-to-all-done = f32[1,2,32,16,128]{4,3,1,0,2:T(8,128)S(1)} async-done(((f32[1,2,32,16,128]{4,3,1,0,2:T(8,128)}), f32[1,2,32,16,128]{4,3,1,0,2:T(8,128)S(1)}, u32[]{:S(2)}, u32[]{:S(2)}) %all-to-all-start) | async-done | bytes 524320 | tf_op jit(solution)/shard_map/all_to_all | solution.py:69
  99.4 2.5 %fusion.2 = (bf16[1,2,16,4096]{3,2,1,0:T(8,128)(2,1)S(1)}, f32[1,2,16,4096]{3,2,1,0:T(8,128)}, f32[1,2,16,4096]{3,2,1,0:T(8,128)}, f32[1,2,16,4096]{3,2,1,0:T(8,128)}) fusion(f32[1,2,16,4096]{3,2,1,0:T(8,128)S(1)} %copy-done.1, f32[]{:T(128)} %bitcast.16, f32[]{:T(128)} %bitcast.13, f32[]{:T(128)} %fusion.1, f32[1,2,16,4096]{3,0,2,1:T(1,128)S(1)} %bitcast.85, ...), kind=kLoop, calls=%fused_computation.27 | loop fusion | flops 1703936 | bytes 4456460 | tf_op jit(solution)/shard_map/convert_element_type | solution.py:82
  102.0 15.8 %all_to_all.10 = bf16[1,2,32,16,128]{4,3,1,0,2:T(8,128)(2,1)S(1)} all-to-all(bf16[1,2,32,16,128]{4,3,1,0,2:T(8,128)(2,1)S(1)} %copy.53), channel_id=1, replica_groups=mesh['dp'=8,'shard'=32] {'shard'}, dimensions={2} | all-to-all | bytes 524288 | tf_op jit(solution)/shard_map/all_to_all | solution.py:84
  117.8 2.8 %collective-permute-start.7 = (bf16[2,512,128]{2,1,0:T(8,128)(2,1)S(1)}, bf16[2,512,128]{2,1,0:T(8,128)(2,1)S(1)}, u32[]{:S(2)}, u32[]{:S(2)}) collective-permute-start(bf16[2,512,128]{2,1,0:T(8,128)(2,1)S(1)} %bitcast.87), channel_id=1, source_target_pairs={{0,32},{32,0},{64,96},{96,64},{128,160},{160,128},{192,224},{224,1... | collective-permute-start | bytes 786440 | tf_op jit(solution)/shard_map/ppermute | solution.py:41
  120.6 6.0 %collective-permute-done.7 = bf16[2,512,128]{2,1,0:T(8,128)(2,1)S(1)} collective-permute-done((bf16[2,512,128]{2,1,0:T(8,128)(2,1)S(1)}, bf16[2,512,128]{2,1,0:T(8,128)(2,1)S(1)}, u32[]{:S(2)}, u32[]{:S(2)}) %collective-permute-start.7) | collective-permute-done | bytes 262176 | tf_op jit(solution)/shard_map/ppermute | solution.py:41
  126.8 3.2 %collective-permute-start.9 = (bf16[2,512,128]{2,1,0:T(8,128)(2,1)S(1)}, bf16[2,512,128]{2,1,0:T(8,128)(2,1)S(1)}, u32[]{:S(2)}, u32[]{:S(2)}) collective-permute-start(bf16[2,512,128]{2,1,0:T(8,128)(2,1)S(1)} %get-tuple-element.15), channel_id=1, source_target_pairs={{0,192},{32,224},{64,0},{96,32},{128,64},{160,96},{192,128},{224,1... | collective-permute-start | bytes 786440 | tf_op jit(solution)/shard_map/ppermute | solution.py:50
  130.5 3.9 %collective-permute-done.8 = bf16[2,512,128]{2,1,0:T(8,128)(2,1)S(1)} collective-permute-done((bf16[2,512,128]{2,1,0:T(8,128)(2,1)S(1)}, bf16[2,512,128]{2,1,0:T(8,128)(2,1)S(1)}, u32[]{:S(2)}, u32[]{:S(2)}) %collective-permute-start.8) | collective-permute-done | bytes 262176 | tf_op jit(solution)/shard_map/ppermute | solution.py:49
  134.4 3.3 %collective-permute-start.11 = (bf16[2,512,128]{2,1,0:T(8,128)(2,1)S(1)}, bf16[2,512,128]{2,1,0:T(8,128)(2,1)S(1)}, u32[]{:S(2)}, u32[]{:S(2)}) collective-permute-start(bf16[2,512,128]{2,1,0:T(8,128)(2,1)S(1)} %collective-permute-done.9), channel_id=1, source_target_pairs={{0,192},{32,224},{64,0},{96,32},{128,64},{160,96},{192,128},{224,1... | collective-permute-start | bytes 786440 | tf_op jit(solution)/shard_map/ppermute | solution.py:50
  137.7 4.5 %collective-permute-done.10 = bf16[2,512,128]{2,1,0:T(8,128)(2,1)S(1)} collective-permute-done((bf16[2,512,128]{2,1,0:T(8,128)(2,1)S(1)}, bf16[2,512,128]{2,1,0:T(8,128)(2,1)S(1)}, u32[]{:S(2)}, u32[]{:S(2)}) %collective-permute-start.10) | collective-permute-done | bytes 262176 | tf_op jit(solution)/shard_map/ppermute | solution.py:49
  142.3 3.6 %collective-permute-start.13 = (bf16[2,512,128]{2,1,0:T(8,128)(2,1)S(1)}, bf16[2,512,128]{2,1,0:T(8,128)(2,1)S(1)}, u32[]{:S(2)}, u32[]{:S(2)}) collective-permute-start(bf16[2,512,128]{2,1,0:T(8,128)(2,1)S(1)} %collective-permute-done.11), channel_id=1, source_target_pairs={{0,192},{32,224},{64,0},{96,32},{128,64},{160,96},{192,128},{224,1... | collective-permute-start | bytes 786440 | tf_op jit(solution)/shard_map/ppermute | solution.py:50
  145.9 3.9 %collective-permute-done.12 = bf16[2,512,128]{2,1,0:T(8,128)(2,1)S(1)} collective-permute-done((bf16[2,512,128]{2,1,0:T(8,128)(2,1)S(1)}, bf16[2,512,128]{2,1,0:T(8,128)(2,1)S(1)}, u32[]{:S(2)}, u32[]{:S(2)}) %collective-permute-start.12) | collective-permute-done | bytes 262176 | tf_op jit(solution)/shard_map/ppermute | solution.py:49
  (43 shorter events, 13.3 us)
Async XLA Ops:
  5.4 14.5 %collective-permute-start.3 = (f32[2,512,128]{2,1,0:T(8,128)}, f32[2,512,128]{2,1,0:T(8,128)S(1)}, u32[]{:S(2)}, u32[]{:S(2)}) collective-permute-start(f32[2,512,128]{2,1,0:T(8,128)} %dynamic-slice_bitcast_fusion), channel_id=1, source_target_pairs={{0,192},{32,224},{64,0},{96,32},{128,64},{160,96},{192,128},{224,1... | collective-permute-start | bytes 1572872 | tf_op jit(solution)/shard_map/ppermute | solution.py:30
  10.3 14.8 %collective-permute-start = (f32[2,512,128]{2,1,0:T(8,128)}, f32[2,512,128]{2,1,0:T(8,128)S(1)}, u32[]{:S(2)}, u32[]{:S(2)}) collective-permute-start(f32[2,512,128]{2,1,0:T(8,128)} %dynamic-slice_bitcast_fusion.1), channel_id=1, source_target_pairs={{0,64},{32,96},{64,128},{96,160},{128,192},{160,224},{192,0},{224,... | collective-permute-start | bytes 1572872 | tf_op jit(solution)/shard_map/ppermute | solution.py:29
  20.8 14.2 %collective-permute-start.4 = (f32[2,512,128]{2,1,0:T(8,128)}, f32[2,512,128]{2,1,0:T(8,128)S(1)}, u32[]{:S(2)}, u32[]{:S(2)}) collective-permute-start(f32[2,512,128]{2,1,0:T(8,128)} %bitcast_add_fusion.2), channel_id=1, source_target_pairs={{0,192},{32,224},{64,0},{96,32},{128,64},{160,96},{192,128},{224,1... | collective-permute-start | bytes 1572872 | tf_op jit(solution)/shard_map/ppermute | solution.py:30
  27.0 13.9 %collective-permute-start.1 = (f32[2,512,128]{2,1,0:T(8,128)}, f32[2,512,128]{2,1,0:T(8,128)S(1)}, u32[]{:S(2)}, u32[]{:S(2)}) collective-permute-start(f32[2,512,128]{2,1,0:T(8,128)} %bitcast_add_fusion.5), channel_id=1, source_target_pairs={{0,64},{32,96},{64,128},{96,160},{128,192},{160,224},{192,0},{224,... | collective-permute-start | bytes 1572872 | tf_op jit(solution)/shard_map/ppermute | solution.py:29
  35.9 13.4 %collective-permute-start.5 = (f32[2,512,128]{2,1,0:T(8,128)}, f32[2,512,128]{2,1,0:T(8,128)S(1)}, u32[]{:S(2)}, u32[]{:S(2)}) collective-permute-start(f32[2,512,128]{2,1,0:T(8,128)} %bitcast_add_fusion.1), channel_id=1, source_target_pairs={{0,192},{32,224},{64,0},{96,32},{128,64},{160,96},{192,128},{224,1... | collective-permute-start | bytes 1572872 | tf_op jit(solution)/shard_map/ppermute | solution.py:30
  42.9 13.1 %collective-permute-start.2 = (f32[2,512,128]{2,1,0:T(8,128)}, f32[2,512,128]{2,1,0:T(8,128)S(1)}, u32[]{:S(2)}, u32[]{:S(2)}) collective-permute-start(f32[2,512,128]{2,1,0:T(8,128)} %bitcast_add_fusion.4), channel_id=1, source_target_pairs={{0,64},{32,96},{64,128},{96,160},{128,192},{160,224},{192,0},{224,... | collective-permute-start | bytes 1572872 | tf_op jit(solution)/shard_map/ppermute | solution.py:29
  57.1 25.5 %copy-start.4 = (f32[64]{0:T(128)S(1)}, f32[64]{0:T(128)}, u32[]{:S(2)}) copy-start(f32[64]{0:T(128)} %param.12) | copy-start | bytes 772
  57.1 12.4 %collective-permute-start.6 = (f32[2,512,128]{2,1,0:T(8,128)S(1)}, f32[2,512,128]{2,1,0:T(8,128)S(1)}, u32[]{:S(2)}, u32[]{:S(2)}) collective-permute-start(f32[2,512,128]{2,1,0:T(8,128)S(1)} %broadcast_select_fusion.2), channel_id=1, source_target_pairs={{0,32},{32,0},{64,96},{96,64},{128,160},{160,128},{192,224},{224,1... | collective-permute-start | bytes 1572872 | tf_op jit(solution)/shard_map/ppermute | solution.py:33
  70.7 28.7 %copy-start.1 = (f32[1,2,16,4096]{3,2,1,0:T(8,128)S(1)}, f32[1,2,16,4096]{3,2,1,0:T(8,128)}, u32[]{:S(2)}) copy-start(f32[1,2,16,4096]{3,2,1,0:T(8,128)} %param.8) | copy-start | bytes 1572868
  70.7 28.7 %copy-start.2 = (f32[1,2,16,4096]{3,2,1,0:T(8,128)S(1)}, f32[1,2,16,4096]{3,2,1,0:T(8,128)}, u32[]{:S(2)}) copy-start(f32[1,2,16,4096]{3,2,1,0:T(8,128)} %param.10) | copy-start | bytes 1572868
  70.7 28.7 %copy-start.3 = (f32[1,2,16,4096]{3,2,1,0:T(8,128)S(1)}, f32[1,2,16,4096]{3,2,1,0:T(8,128)}, u32[]{:S(2)}) copy-start(f32[1,2,16,4096]{3,2,1,0:T(8,128)} %param.9) | copy-start | bytes 1572868
  71.6 27.4 %all-to-all-start = ((f32[1,2,32,16,128]{4,3,1,0,2:T(8,128)}), f32[1,2,32,16,128]{4,3,1,0,2:T(8,128)S(1)}, u32[]{:S(2)}, u32[]{:S(2)}) async-start(f32[1,2,32,16,128]{4,3,1,0,2:T(8,128)} %copy.47), calls=%async_computation | async-start | bytes 1048576 | tf_op jit(solution)/shard_map/all_to_all | solution.py:69
  117.8 8.8 %collective-permute-start.7 = (bf16[2,512,128]{2,1,0:T(8,128)(2,1)S(1)}, bf16[2,512,128]{2,1,0:T(8,128)(2,1)S(1)}, u32[]{:S(2)}, u32[]{:S(2)}) collective-permute-start(bf16[2,512,128]{2,1,0:T(8,128)(2,1)S(1)} %bitcast.87), channel_id=1, source_target_pairs={{0,32},{32,0},{64,96},{96,64},{128,160},{160,128},{192,224},{224,1... | collective-permute-start | bytes 786440 | tf_op jit(solution)/shard_map/ppermute | solution.py:41
  126.7 7.7 %collective-permute-start.8 = (bf16[2,512,128]{2,1,0:T(8,128)(2,1)S(1)}, bf16[2,512,128]{2,1,0:T(8,128)(2,1)S(1)}, u32[]{:S(2)}, u32[]{:S(2)}) collective-permute-start(bf16[2,512,128]{2,1,0:T(8,128)(2,1)S(1)} %get-tuple-element.14), channel_id=1, source_target_pairs={{0,64},{32,96},{64,128},{96,160},{128,192},{160,224},{192,0},{224,... | collective-permute-start | bytes 786440 | tf_op jit(solution)/shard_map/ppermute | solution.py:49
  126.8 7.6 %collective-permute-start.9 = (bf16[2,512,128]{2,1,0:T(8,128)(2,1)S(1)}, bf16[2,512,128]{2,1,0:T(8,128)(2,1)S(1)}, u32[]{:S(2)}, u32[]{:S(2)}) collective-permute-start(bf16[2,512,128]{2,1,0:T(8,128)(2,1)S(1)} %get-tuple-element.15), channel_id=1, source_target_pairs={{0,192},{32,224},{64,0},{96,32},{128,64},{160,96},{192,128},{224,1... | collective-permute-start | bytes 786440 | tf_op jit(solution)/shard_map/ppermute | solution.py:50
  134.3 7.9 %collective-permute-start.10 = (bf16[2,512,128]{2,1,0:T(8,128)(2,1)S(1)}, bf16[2,512,128]{2,1,0:T(8,128)(2,1)S(1)}, u32[]{:S(2)}, u32[]{:S(2)}) collective-permute-start(bf16[2,512,128]{2,1,0:T(8,128)(2,1)S(1)} %collective-permute-done.8), channel_id=1, source_target_pairs={{0,64},{32,96},{64,128},{96,160},{128,192},{160,224},{192,0},{224,... | collective-permute-start | bytes 786440 | tf_op jit(solution)/shard_map/ppermute | solution.py:49
  134.4 7.9 %collective-permute-start.11 = (bf16[2,512,128]{2,1,0:T(8,128)(2,1)S(1)}, bf16[2,512,128]{2,1,0:T(8,128)(2,1)S(1)}, u32[]{:S(2)}, u32[]{:S(2)}) collective-permute-start(bf16[2,512,128]{2,1,0:T(8,128)(2,1)S(1)} %collective-permute-done.9), channel_id=1, source_target_pairs={{0,192},{32,224},{64,0},{96,32},{128,64},{160,96},{192,128},{224,1... | collective-permute-start | bytes 786440 | tf_op jit(solution)/shard_map/ppermute | solution.py:50
  142.3 7.6 %collective-permute-start.12 = (bf16[2,512,128]{2,1,0:T(8,128)(2,1)S(1)}, bf16[2,512,128]{2,1,0:T(8,128)(2,1)S(1)}, u32[]{:S(2)}, u32[]{:S(2)}) collective-permute-start(bf16[2,512,128]{2,1,0:T(8,128)(2,1)S(1)} %collective-permute-done.10), channel_id=1, source_target_pairs={{0,64},{32,96},{64,128},{96,160},{128,192},{160,224},{192,0},{224,... | collective-permute-start | bytes 786440 | tf_op jit(solution)/shard_map/ppermute | solution.py:49
  142.3 7.7 %collective-permute-start.13 = (bf16[2,512,128]{2,1,0:T(8,128)(2,1)S(1)}, bf16[2,512,128]{2,1,0:T(8,128)(2,1)S(1)}, u32[]{:S(2)}, u32[]{:S(2)}) collective-permute-start(bf16[2,512,128]{2,1,0:T(8,128)(2,1)S(1)} %collective-permute-done.11), channel_id=1, source_target_pairs={{0,192},{32,224},{64,0},{96,32},{128,64},{160,96},{192,128},{224,1... | collective-permute-start | bytes 786440 | tf_op jit(solution)/shard_map/ppermute | solution.py:50
  150.1 1.3 copy-start

commit v3 on v2

--- a/solution.py
+++ b/solution.py
@@ -16,21 +16,34 @@
     return lax.dynamic_index_in_dim(x, index, axis=1, keepdims=False)
 
 
+def _ring_sum(chunks, y, ring, perm, sign):
+    acc = _take(chunks, (y - sign) % ring)
+    for t in range(ring - 1):
+        acc = lax.ppermute(acc, "dp", perm) + _take(chunks, (y - sign * (t + 2)) % ring)
+    return acc
+
+
 def _reduce_scatter_dp(x, groups):
     ring, plus, minus, partner = _dp_rings(groups)
     d = lax.axis_index("dp")
     y = d // 2
     h = d % 2
-    even = x[:, :, 0]
-    odd = x[:, :, 1]
-    up = _take(even, (y - 1) % ring)
-    down = _take(odd, (y + 1) % ring)
-    for t in range(ring - 1):
-        up = lax.ppermute(up, "dp", plus) + _take(even, (y - t - 2) % ring)
-        down = lax.ppermute(down, "dp", minus) + _take(odd, (y + t + 2) % ring)
+    half = x.shape[0] // 2
+    rows = x.shape[3] // 2
+    first = x[:half]
+    up = _ring_sum(first[:, :, 0], y, ring, plus, 1)
+    down = _ring_sum(first[:, :, 1], y, ring, minus, -1)
     keep = lax.select(h == 0, up, down)
     send = lax.select(h == 0, down, up)
-    return keep + lax.ppermute(send, "dp", partner)
+    done_first = keep + lax.ppermute(send, "dp", partner)
+    second = x[half:]
+    mine = lax.select(h == 0, second[:, :, 0], second[:, :, 1])
+    theirs = lax.select(h == 0, second[:, :, 1], second[:, :, 0])
+    paired = mine + lax.ppermute(theirs, "dp", partner)
+    top = _ring_sum(paired[:, :, :rows], y, ring, plus, 1)
+    bottom = _ring_sum(paired[:, :, rows:], y, ring, minus, -1)
+    done_second = jnp.concatenate([top, bottom], axis=1)
+    return jnp.concatenate([done_first, done_second], axis=0)
 
 
 def _all_gather_dp(mine, groups):
@@ -38,11 +51,14 @@
     d = lax.axis_index("dp")
     y = d // 2
     h = d % 2
-    other = lax.ppermute(mine, "dp", partner)
-    even = lax.select(h == 0, mine, other)
-    odd = lax.select(h == 0, other, mine)
     lead, block, cols = mine.shape
-    out = jnp.zeros((lead, ring, 2, block, cols), mine.dtype)
+    half = lead // 2
+    rows = block // 2
+    first = mine[:half]
+    other = lax.ppermute(first, "dp", partner)
+    even = lax.select(h == 0, first, other)
+    odd = lax.select(h == 0, other, first)
+    out = jnp.zeros((half, ring, 2, block, cols), mine.dtype)
     out = lax.dynamic_update_slice(out, jnp.stack([even, odd], axis=1)[:, None], (0, y, 0, 0, 0))
     up, down = even, odd
     for t in range(ring - 1):
@@ -50,7 +66,22 @@
         down = lax.ppermute(down, "dp", minus)
         out = lax.dynamic_update_slice(out, up[:, None, None], (0, (y - t - 1) % ring, 0, 0, 0))
         out = lax.dynamic_update_slice(out, down[:, None, None], (0, (y + t + 1) % ring, 1, 0, 0))
-    return out.reshape(lead, groups * block, cols)
+    panel_first = out.reshape(half, groups * block, cols)
+    second = mine[half:]
+    ours = jnp.zeros((lead - half, ring, block, cols), mine.dtype)
+    ours = lax.dynamic_update_slice(ours, second[:, None], (0, y, 0, 0))
+    top = second[:, :rows]
+    bottom = second[:, rows:]
+    for t in range(ring - 1):
+        top = lax.ppermute(top, "dp", plus)
+        bottom = lax.ppermute(bottom, "dp", minus)
+        ours = lax.dynamic_update_slice(ours, top[:, None], (0, (y - t - 1) % ring, 0, 0))
+        ours = lax.dynamic_update_slice(ours, bottom[:, None], (0, (y + t + 1) % ring, rows, 0))
+    others = lax.ppermute(ours, "dp", partner)
+    even = lax.select(h == 0, ours, others)
+    odd = lax.select(h == 0, others, ours)
+    panel_second = jnp.stack([even, odd], axis=2).reshape(lead - half, groups * block, cols)
+    return jnp.concatenate([panel_first, panel_second], axis=0)
 
 
 def body(grads, params, moment_one, moment_two, relation_ids, rates, step_count):

time: 153 us -> 151 us (0.987)
  starting transfers between devices: 36 us -> 64.1 us
  waiting for transfers between devices: 76.2 us -> 58.6 us
  blocking collectives: 15.8 us -> 0 us
  other arithmetic: 11.4 us -> 16.2 us
  local copies, waits for them, and re-layouts: 9.77 us -> 7.61 us
    ppermute x8 -> x22, starting transfers between devices: 16.1 us -> 40.8 us  [the longest x12 20.9 us: _ring_sum(): lax.ppermute(acc, 'dp', perm) + _take(chunks, (y - sign * (t + 2)) % ring)]
    ppermute x8 -> x22, waiting for transfers between devices: 48.3 us -> 24.3 us  [the longest x12 20.3 us: _ring_sum(): lax.ppermute(acc, 'dp', perm) + _take(chunks, (y - sign * (t + 2)) % ring)]
    all_to_all x1 -> x0, blocking collectives: 15.8 us -> none  [body(): lax.all_to_all(fresh, 'shard', split_axis=2, concat_axis=2, tiled=True)]
    all_to_all x0 -> x1, waiting for transfers between devices: none -> 12.2 us  [body(): lax.all_to_all(fresh, 'shard', split_axis=2, concat_axis=2, tiled=True)]
    ppermute x3, waiting for transfers between devices: 12.3 us -> 6.41 us  [_all_gather_dp(): up = lax.ppermute(up, 'dp', plus)]
    all_to_all x0 -> x1, starting transfers between devices: none -> 4.45 us  [body(): lax.all_to_all(fresh, 'shard', split_axis=2, concat_axis=2, tiled=True)]
    add x5 -> x12, other arithmetic: 6.63 us -> 8.75 us  [the longest x10 6.29 us: _ring_sum(): lax.ppermute(acc, 'dp', perm) + _take(chunks, (y - sign * (t + 2)) % ring)]
    slice x1 -> x5, local copies, waits for them, and re-layouts: 3.95 us -> 3.73 us  [the longest x1 2.49 us: _reduce_scatter_dp(): first = x[:half]]
  transfers between devices with their start and end apart: 15 -> 30, of which waited for: 12 -> 14; matrix products, arithmetic and copies ran while one was open for 6% -> 9% of each run, Pallas kernels for 0% -> 0%
where the time goes in v3:
time: 151 us; the launch traced here: 149 us
  starting transfers between devices  64.1 us (42%)
  waiting for transfers between devices  58.6 us (39%)
  other arithmetic  16.2 us (11%)
  local copies, waits for them, and re-layouts  7.61 us (5%)
  between operations  2.46 us (2%)
    ppermute x12, starting transfers between devices, _ring_sum(): lax.ppermute(acc, 'dp', perm) + _take(chunks, (y - sign * (t + 2)) % ring)  20.9 us
    ppermute x12, waiting for transfers between devices, _ring_sum(): lax.ppermute(acc, 'dp', perm) + _take(chunks, (y - sign * (t + 2)) % ring)  20.3 us
    all_to_all x1, waiting for transfers between devices, body(): lax.all_to_all(pieces, 'shard', split_axis=2, concat_axis=2, tiled=True)  15.7 us
    all_to_all x1, waiting for transfers between devices, body(): lax.all_to_all(fresh, 'shard', split_axis=2, concat_axis=2, tiled=True)  12.2 us
    ppermute x3, starting transfers between devices, _all_gather_dp(): bottom = lax.ppermute(bottom, 'dp', minus)  9.99 us
    ppermute x3, starting transfers between devices, _all_gather_dp(): down = lax.ppermute(down, 'dp', minus)  9.91 us
    all_to_all x1, starting transfers between devices, body(): lax.all_to_all(pieces, 'shard', split_axis=2, concat_axis=2, tiled=True)  8.76 us
    ppermute x3, waiting for transfers between devices, _all_gather_dp(): up = lax.ppermute(up, 'dp', plus)  6.41 us
  transfers between devices with their start and end apart: 30, of which 14 were waited for; matrix products, arithmetic and copies ran while one was open for 9% of the time, Pallas kernels for 0%

profile of v3, /device:TPU:32, one launch (start us, length us, event | category | flops | bytes accessed | tf_op | source)
XLA Modules:
  0.0 148.9 jit_solution(257722696982842011)
XLA Ops:
  4.3 3.1 %collective-permute-start.3 = (f32[1,512,128]{2,1,0:T(8,128)S(1)}, f32[1,512,128]{2,1,0:T(8,128)}, u32[]{:S(2)}, u32[]{:S(2)}) collective-permute-start(f32[1,512,128]{2,1,0:T(8,128)S(1)} %dynamic-slice_bitcast_fusion), channel_id=1, source_target_pairs={{0,192},{32,224},{64,0},{96,32},{128,64},{160,96},{192,128},{224,1... | collective-permute-start | bytes 786440 | tf_op jit(solution)/shard_map/ppermute | solution.py:22
  10.2 3.0 %collective-permute-start.7 = (f32[1,4,512,128]{3,2,1,0:T(8,128)}, f32[1,4,512,128]{3,2,1,0:T(8,128)}, u32[]{:S(2)}, u32[]{:S(2)}) collective-permute-start(f32[1,4,512,128]{3,2,1,0:T(8,128)} %select_bitcast_fusion), channel_id=1, source_target_pairs={{0,32},{32,0},{64,96},{96,64},{128,160},{160,128},{192,224},{224,1... | collective-permute-start | bytes 3145736 | tf_op jit(solution)/shard_map/ppermute | solution.py:42
  14.2 3.7 %collective-permute-start.4 = (f32[1,512,128]{2,1,0:T(8,128)S(1)}, f32[1,512,128]{2,1,0:T(8,128)}, u32[]{:S(2)}, u32[]{:S(2)}) collective-permute-start(f32[1,512,128]{2,1,0:T(8,128)S(1)} %bitcast_add_fusion.3), channel_id=1, source_target_pairs={{0,192},{32,224},{64,0},{96,32},{128,64},{160,96},{192,128},{224,1... | collective-permute-start | bytes 786440 | tf_op jit(solution)/shard_map/ppermute | solution.py:22
  24.2 3.8 %collective-permute-start.5 = (f32[1,512,128]{2,1,0:T(8,128)}, f32[1,512,128]{2,1,0:T(8,128)S(1)}, u32[]{:S(2)}, u32[]{:S(2)}) collective-permute-start(f32[1,512,128]{2,1,0:T(8,128)} %bitcast_add_fusion.2), channel_id=1, source_target_pairs={{0,192},{32,224},{64,0},{96,32},{128,64},{160,96},{192,128},{224,1... | collective-permute-start | bytes 786440 | tf_op jit(solution)/shard_map/ppermute | solution.py:22
  32.2 6.0 %collective-permute-done.2 = f32[1,512,128]{2,1,0:T(8,128)} collective-permute-done((f32[1,512,128]{2,1,0:T(8,128)}, f32[1,512,128]{2,1,0:T(8,128)}, u32[]{:S(2)}, u32[]{:S(2)}) %collective-permute-start.2) | collective-permute-done | bytes 262176 | tf_op jit(solution)/shard_map/ppermute | solution.py:22
  39.3 3.1 %collective-permute-start.6 = (f32[1,512,128]{2,1,0:T(8,128)S(1)}, f32[1,512,128]{2,1,0:T(8,128)S(1)}, u32[]{:S(2)}, u32[]{:S(2)}) collective-permute-start(f32[1,512,128]{2,1,0:T(8,128)S(1)} %broadcast_select_fusion.2), channel_id=1, source_target_pairs={{0,32},{32,0},{64,96},{96,64},{128,160},{160,128},{192,224},{224,1... | collective-permute-start | bytes 786440 | tf_op jit(solution)/shard_map/ppermute | solution.py:38
  44.0 3.3 %collective-permute-start.11 = (f32[1,256,128]{2,1,0:T(8,128)S(1)}, f32[1,256,128]{2,1,0:T(8,128)S(1)}, u32[]{:S(2)}, u32[]{:S(2)}) collective-permute-start(f32[1,256,128]{2,1,0:T(8,128)S(1)} %dynamic-slice_bitcast_fusion.2), channel_id=1, source_target_pairs={{0,192},{32,224},{64,0},{96,32},{128,64},{160,96},{192,128},{224,1... | collective-permute-start | bytes 393224 | tf_op jit(solution)/shard_map/ppermute | solution.py:22
  50.7 3.5 %collective-permute-start.12 = (f32[1,256,128]{2,1,0:T(8,128)S(1)}, f32[1,256,128]{2,1,0:T(8,128)S(1)}, u32[]{:S(2)}, u32[]{:S(2)}) collective-permute-start(f32[1,256,128]{2,1,0:T(8,128)S(1)} %bitcast_add_fusion.9), channel_id=1, source_target_pairs={{0,192},{32,224},{64,0},{96,32},{128,64},{160,96},{192,128},{224,1... | collective-permute-start | bytes 393224 | tf_op jit(solution)/shard_map/ppermute | solution.py:22
  54.2 3.9 %collective-permute-done.9 = f32[1,256,128]{2,1,0:T(8,128)S(1)} collective-permute-done((f32[1,256,128]{2,1,0:T(8,128)S(1)}, f32[1,256,128]{2,1,0:T(8,128)S(1)}, u32[]{:S(2)}, u32[]{:S(2)}) %collective-permute-start.9) | collective-permute-done | bytes 131104 | tf_op jit(solution)/shard_map/ppermute | solution.py:22
  58.3 3.3 %collective-permute-start.13 = (f32[1,256,128]{2,1,0:T(8,128)S(1)}, f32[1,256,128]{2,1,0:T(8,128)S(1)}, u32[]{:S(2)}, u32[]{:S(2)}) collective-permute-start(f32[1,256,128]{2,1,0:T(8,128)S(1)} %bitcast_add_fusion.8), channel_id=1, source_target_pairs={{0,192},{32,224},{64,0},{96,32},{128,64},{160,96},{192,128},{224,1... | collective-permute-start | bytes 393224 | tf_op jit(solution)/shard_map/ppermute | solution.py:22
  61.6 2.8 %collective-permute-done.10 = f32[1,256,128]{2,1,0:T(8,128)S(1)} collective-permute-done((f32[1,256,128]{2,1,0:T(8,128)S(1)}, f32[1,256,128]{2,1,0:T(8,128)S(1)}, u32[]{:S(2)}, u32[]{:S(2)}) %collective-permute-start.10) | collective-permute-done | bytes 131104 | tf_op jit(solution)/shard_map/ppermute | solution.py:22
  65.4 8.8 %all-to-all-start = ((f32[1,2,32,16,128]{4,3,1,0,2:T(8,128)}), f32[1,2,32,16,128]{4,3,1,0,2:T(8,128)S(1)}, u32[]{:S(2)}, u32[]{:S(2)}) async-start(f32[1,2,32,16,128]{4,3,1,0,2:T(8,128)} %copy.45), calls=%async_computation | async-start | bytes 1048576 | tf_op jit(solution)/shard_map/all_to_all | solution.py:100
  76.2 15.7 %all-to-all-done = f32[1,2,32,16,128]{4,3,1,0,2:T(8,128)S(1)} async-done(((f32[1,2,32,16,128]{4,3,1,0,2:T(8,128)}), f32[1,2,32,16,128]{4,3,1,0,2:T(8,128)S(1)}, u32[]{:S(2)}, u32[]{:S(2)}) %all-to-all-start) | async-done | bytes 524320 | tf_op jit(solution)/shard_map/all_to_all | solution.py:100
  92.3 2.5 %fusion.2 = (bf16[1,2,16,4096]{3,2,1,0:T(8,128)(2,1)S(1)}, f32[1,2,16,4096]{3,2,1,0:T(8,128)}, f32[1,2,16,4096]{3,2,1,0:T(8,128)}, f32[1,2,16,4096]{3,2,1,0:T(8,128)}) fusion(f32[1,2,16,4096]{3,2,1,0:T(8,128)S(1)} %copy-done, f32[]{:T(128)} %bitcast.27, f32[]{:T(128)} %bitcast.24, f32[]{:T(128)} %fusion.1, f32[1,2,16,4096]{3,0,2,1:T(1,128)S(1)} %bitcast.126, ...), kind=kLoop, calls=%fused_computation.51 | loop fusion | flops 1703936 | bytes 4456460 | tf_op jit(solution)/shard_map/convert_element_type | solution.py:113
  95.7 4.5 %all-to-all-start.1 = ((bf16[1,2,32,16,128]{4,3,1,0,2:T(8,128)(2,1)}), bf16[1,2,32,16,128]{4,3,1,0,2:T(8,128)(2,1)S(1)}, u32[]{:S(2)}, u32[]{:S(2)}) async-start(bf16[1,2,32,16,128]{4,3,1,0,2:T(8,128)(2,1)} %copy.51), calls=%async_computation.1 | async-start | bytes 524288 | tf_op jit(solution)/shard_map/all_to_all | solution.py:115
  100.2 12.2 %all-to-all-done.1 = bf16[1,2,32,16,128]{4,3,1,0,2:T(8,128)(2,1)S(1)} async-done(((bf16[1,2,32,16,128]{4,3,1,0,2:T(8,128)(2,1)}), bf16[1,2,32,16,128]{4,3,1,0,2:T(8,128)(2,1)S(1)}, u32[]{:S(2)}, u32[]{:S(2)}) %all-to-all-start.1) | async-done | bytes 262176 | tf_op jit(solution)/shard_map/all_to_all | solution.py:115
  114.6 3.4 %collective-permute-start.22 = (bf16[1,256,128]{2,1,0:T(8,128)(2,1)S(1)}, bf16[1,256,128]{2,1,0:T(8,128)(2,1)S(1)}, u32[]{:S(2)}, u32[]{:S(2)}) collective-permute-start(bf16[1,256,128]{2,1,0:T(8,128)(2,1)S(1)} %get-tuple-element.26), channel_id=1, source_target_pairs={{0,192},{32,224},{64,0},{96,32},{128,64},{160,96},{192,128},{224,1... | collective-permute-start | bytes 196616 | tf_op jit(solution)/shard_map/ppermute | solution.py:77
  120.1 3.3 %collective-permute-start.24 = (bf16[1,256,128]{2,1,0:T(8,128)(2,1)S(1)}, bf16[1,256,128]{2,1,0:T(8,128)(2,1)S(1)}, u32[]{:S(2)}, u32[]{:S(2)}) collective-permute-start(bf16[1,256,128]{2,1,0:T(8,128)(2,1)S(1)} %collective-permute-done.22), channel_id=1, source_target_pairs={{0,192},{32,224},{64,0},{96,32},{128,64},{160,96},{192,128},{224,1... | collective-permute-start | bytes 196616 | tf_op jit(solution)/shard_map/ppermute | solution.py:77
  123.6 3.2 %collective-permute-start.16 = (bf16[1,512,128]{2,1,0:T(8,128)(2,1)S(1)}, bf16[1,512,128]{2,1,0:T(8,128)(2,1)S(1)}, u32[]{:S(2)}, u32[]{:S(2)}) collective-permute-start(bf16[1,512,128]{2,1,0:T(8,128)(2,1)S(1)} %get-tuple-element.23), channel_id=1, source_target_pairs={{0,192},{32,224},{64,0},{96,32},{128,64},{160,96},{192,128},{224,1... | collective-permute-start | bytes 393224 | tf_op jit(solution)/shard_map/ppermute | solution.py:66
  126.9 3.3 %collective-permute-start.26 = (bf16[1,256,128]{2,1,0:T(8,128)(2,1)S(1)}, bf16[1,256,128]{2,1,0:T(8,128)(2,1)S(1)}, u32[]{:S(2)}, u32[]{:S(2)}) collective-permute-start(bf16[1,256,128]{2,1,0:T(8,128)(2,1)S(1)} %collective-permute-done.24), channel_id=1, source_target_pairs={{0,192},{32,224},{64,0},{96,32},{128,64},{160,96},{192,128},{224,1... | collective-permute-start | bytes 196616 | tf_op jit(solution)/shard_map/ppermute | solution.py:77
  134.0 3.4 %collective-permute-start.18 = (bf16[1,512,128]{2,1,0:T(8,128)(2,1)S(1)}, bf16[1,512,128]{2,1,0:T(8,128)(2,1)S(1)}, u32[]{:S(2)}, u32[]{:S(2)}) collective-permute-start(bf16[1,512,128]{2,1,0:T(8,128)(2,1)S(1)} %collective-permute-done.16), channel_id=1, source_target_pairs={{0,192},{32,224},{64,0},{96,32},{128,64},{160,96},{192,128},{224,1... | collective-permute-start | bytes 393224 | tf_op jit(solution)/shard_map/ppermute | solution.py:66
  137.4 3.6 %collective-permute-done.17 = bf16[1,512,128]{2,1,0:T(8,128)(2,1)S(1)} collective-permute-done((bf16[1,512,128]{2,1,0:T(8,128)(2,1)S(1)}, bf16[1,512,128]{2,1,0:T(8,128)(2,1)S(1)}, u32[]{:S(2)}, u32[]{:S(2)}) %collective-permute-start.17) | collective-permute-done | bytes 131104 | tf_op jit(solution)/shard_map/ppermute | solution.py:65
  141.0 3.3 %collective-permute-start.20 = (bf16[1,512,128]{2,1,0:T(8,128)(2,1)S(1)}, bf16[1,512,128]{2,1,0:T(8,128)(2,1)S(1)}, u32[]{:S(2)}, u32[]{:S(2)}) collective-permute-start(bf16[1,512,128]{2,1,0:T(8,128)(2,1)S(1)} %collective-permute-done.18), channel_id=1, source_target_pairs={{0,192},{32,224},{64,0},{96,32},{128,64},{160,96},{192,128},{224,1... | collective-permute-start | bytes 393224 | tf_op jit(solution)/shard_map/ppermute | solution.py:66
  144.4 2.8 %collective-permute-done.19 = bf16[1,512,128]{2,1,0:T(8,128)(2,1)S(1)} collective-permute-done((bf16[1,512,128]{2,1,0:T(8,128)(2,1)S(1)}, bf16[1,512,128]{2,1,0:T(8,128)(2,1)S(1)}, u32[]{:S(2)}, u32[]{:S(2)}) %collective-permute-start.19) | collective-permute-done | bytes 131104 | tf_op jit(solution)/shard_map/ppermute | solution.py:65
  (94 shorter events, 37.0 us)
Async XLA Ops:
  4.3 8.9 %collective-permute-start.3 = (f32[1,512,128]{2,1,0:T(8,128)S(1)}, f32[1,512,128]{2,1,0:T(8,128)}, u32[]{:S(2)}, u32[]{:S(2)}) collective-permute-start(f32[1,512,128]{2,1,0:T(8,128)S(1)} %dynamic-slice_bitcast_fusion), channel_id=1, source_target_pairs={{0,192},{32,224},{64,0},{96,32},{128,64},{160,96},{192,128},{224,1... | collective-permute-start | bytes 786440 | tf_op jit(solution)/shard_map/ppermute | solution.py:22
  9.1 9.3 %collective-permute-start = (f32[1,512,128]{2,1,0:T(8,128)}, f32[1,512,128]{2,1,0:T(8,128)}, u32[]{:S(2)}, u32[]{:S(2)}) collective-permute-start(f32[1,512,128]{2,1,0:T(8,128)} %dynamic-slice_bitcast_fusion.1), channel_id=1, source_target_pairs={{0,64},{32,96},{64,128},{96,160},{128,192},{160,224},{192,0},{224,... | collective-permute-start | bytes 786440 | tf_op jit(solution)/shard_map/ppermute | solution.py:22
  10.2 32.3 %collective-permute-start.7 = (f32[1,4,512,128]{3,2,1,0:T(8,128)}, f32[1,4,512,128]{3,2,1,0:T(8,128)}, u32[]{:S(2)}, u32[]{:S(2)}) collective-permute-start(f32[1,4,512,128]{3,2,1,0:T(8,128)} %select_bitcast_fusion), channel_id=1, source_target_pairs={{0,32},{32,0},{64,96},{96,64},{128,160},{160,128},{192,224},{224,1... | collective-permute-start | bytes 3145736 | tf_op jit(solution)/shard_map/ppermute | solution.py:42
  14.2 8.4 %collective-permute-start.4 = (f32[1,512,128]{2,1,0:T(8,128)S(1)}, f32[1,512,128]{2,1,0:T(8,128)}, u32[]{:S(2)}, u32[]{:S(2)}) collective-permute-start(f32[1,512,128]{2,1,0:T(8,128)S(1)} %bitcast_add_fusion.3), channel_id=1, source_target_pairs={{0,192},{32,224},{64,0},{96,32},{128,64},{160,96},{192,128},{224,1... | collective-permute-start | bytes 786440 | tf_op jit(solution)/shard_map/ppermute | solution.py:22
  20.1 8.4 %collective-permute-start.1 = (f32[1,512,128]{2,1,0:T(8,128)}, f32[1,512,128]{2,1,0:T(8,128)}, u32[]{:S(2)}, u32[]{:S(2)}) collective-permute-start(f32[1,512,128]{2,1,0:T(8,128)} %bitcast_add_fusion.6), channel_id=1, source_target_pairs={{0,64},{32,96},{64,128},{96,160},{128,192},{160,224},{192,0},{224,... | collective-permute-start | bytes 786440 | tf_op jit(solution)/shard_map/ppermute | solution.py:22
  24.2 8.0 %collective-permute-start.5 = (f32[1,512,128]{2,1,0:T(8,128)}, f32[1,512,128]{2,1,0:T(8,128)S(1)}, u32[]{:S(2)}, u32[]{:S(2)}) collective-permute-start(f32[1,512,128]{2,1,0:T(8,128)} %bitcast_add_fusion.2), channel_id=1, source_target_pairs={{0,192},{32,224},{64,0},{96,32},{128,64},{160,96},{192,128},{224,1... | collective-permute-start | bytes 786440 | tf_op jit(solution)/shard_map/ppermute | solution.py:22
  30.3 7.9 %collective-permute-start.2 = (f32[1,512,128]{2,1,0:T(8,128)}, f32[1,512,128]{2,1,0:T(8,128)}, u32[]{:S(2)}, u32[]{:S(2)}) collective-permute-start(f32[1,512,128]{2,1,0:T(8,128)} %bitcast_add_fusion.5), channel_id=1, source_target_pairs={{0,64},{32,96},{64,128},{96,160},{128,192},{160,224},{192,0},{224,... | collective-permute-start | bytes 786440 | tf_op jit(solution)/shard_map/ppermute | solution.py:22
  39.3 8.0 %collective-permute-start.6 = (f32[1,512,128]{2,1,0:T(8,128)S(1)}, f32[1,512,128]{2,1,0:T(8,128)S(1)}, u32[]{:S(2)}, u32[]{:S(2)}) collective-permute-start(f32[1,512,128]{2,1,0:T(8,128)S(1)} %broadcast_select_fusion.2), channel_id=1, source_target_pairs={{0,32},{32,0},{64,96},{96,64},{128,160},{160,128},{192,224},{224,1... | collective-permute-start | bytes 786440 | tf_op jit(solution)/shard_map/ppermute | solution.py:38
  43.9 6.7 %collective-permute-start.8 = (f32[1,256,128]{2,1,0:T(8,128)S(1)}, f32[1,256,128]{2,1,0:T(8,128)S(1)}, u32[]{:S(2)}, u32[]{:S(2)}) collective-permute-start(f32[1,256,128]{2,1,0:T(8,128)S(1)} %dynamic-slice_bitcast_fusion.3), channel_id=1, source_target_pairs={{0,64},{32,96},{64,128},{96,160},{128,192},{160,224},{192,0},{224,... | collective-permute-start | bytes 393224 | tf_op jit(solution)/shard_map/ppermute | solution.py:22
  44.0 6.6 %collective-permute-start.11 = (f32[1,256,128]{2,1,0:T(8,128)S(1)}, f32[1,256,128]{2,1,0:T(8,128)S(1)}, u32[]{:S(2)}, u32[]{:S(2)}) collective-permute-start(f32[1,256,128]{2,1,0:T(8,128)S(1)} %dynamic-slice_bitcast_fusion.2), channel_id=1, source_target_pairs={{0,192},{32,224},{64,0},{96,32},{128,64},{160,96},{192,128},{224,1... | collective-permute-start | bytes 393224 | tf_op jit(solution)/shard_map/ppermute | solution.py:22
  50.6 7.5 %collective-permute-start.9 = (f32[1,256,128]{2,1,0:T(8,128)S(1)}, f32[1,256,128]{2,1,0:T(8,128)S(1)}, u32[]{:S(2)}, u32[]{:S(2)}) collective-permute-start(f32[1,256,128]{2,1,0:T(8,128)S(1)} %bitcast_add_fusion.12), channel_id=1, source_target_pairs={{0,64},{32,96},{64,128},{96,160},{128,192},{160,224},{192,0},{224,... | collective-permute-start | bytes 393224 | tf_op jit(solution)/shard_map/ppermute | solution.py:22
  50.7 7.5 %collective-permute-start.12 = (f32[1,256,128]{2,1,0:T(8,128)S(1)}, f32[1,256,128]{2,1,0:T(8,128)S(1)}, u32[]{:S(2)}, u32[]{:S(2)}) collective-permute-start(f32[1,256,128]{2,1,0:T(8,128)S(1)} %bitcast_add_fusion.9), channel_id=1, source_target_pairs={{0,192},{32,224},{64,0},{96,32},{128,64},{160,96},{192,128},{224,1... | collective-permute-start | bytes 393224 | tf_op jit(solution)/shard_map/ppermute | solution.py:22
  58.1 6.3 %collective-permute-start.10 = (f32[1,256,128]{2,1,0:T(8,128)S(1)}, f32[1,256,128]{2,1,0:T(8,128)S(1)}, u32[]{:S(2)}, u32[]{:S(2)}) collective-permute-start(f32[1,256,128]{2,1,0:T(8,128)S(1)} %bitcast_add_fusion.11), channel_id=1, source_target_pairs={{0,64},{32,96},{64,128},{96,160},{128,192},{160,224},{192,0},{224,... | collective-permute-start | bytes 393224 | tf_op jit(solution)/shard_map/ppermute | solution.py:22
  65.4 26.5 %all-to-all-start = ((f32[1,2,32,16,128]{4,3,1,0,2:T(8,128)}), f32[1,2,32,16,128]{4,3,1,0,2:T(8,128)S(1)}, u32[]{:S(2)}, u32[]{:S(2)}) async-start(f32[1,2,32,16,128]{4,3,1,0,2:T(8,128)} %copy.45), calls=%async_computation | async-start | bytes 1048576 | tf_op jit(solution)/shard_map/all_to_all | solution.py:100
  95.7 16.7 %all-to-all-start.1 = ((bf16[1,2,32,16,128]{4,3,1,0,2:T(8,128)(2,1)}), bf16[1,2,32,16,128]{4,3,1,0,2:T(8,128)(2,1)S(1)}, u32[]{:S(2)}, u32[]{:S(2)}) async-start(bf16[1,2,32,16,128]{4,3,1,0,2:T(8,128)(2,1)} %copy.51), calls=%async_computation.1 | async-start | bytes 524288 | tf_op jit(solution)/shard_map/all_to_all | solution.py:115
  112.4 11.1 %collective-permute-start.14 = (bf16[1,512,128]{2,1,0:T(8,128)(2,1)S(1)}, bf16[1,512,128]{2,1,0:T(8,128)(2,1)S(1)}, u32[]{:S(2)}, u32[]{:S(2)}) collective-permute-start(bf16[1,512,128]{2,1,0:T(8,128)(2,1)S(1)} %bitcast.133), channel_id=1, source_target_pairs={{0,32},{32,0},{64,96},{96,64},{128,160},{160,128},{192,224},{224,1... | collective-permute-start | bytes 393224 | tf_op jit(solution)/shard_map/ppermute | solution.py:58
  120.1 6.7 %collective-permute-start.23 = (bf16[1,256,128]{2,1,0:T(8,128)(2,1)S(1)}, bf16[1,256,128]{2,1,0:T(8,128)(2,1)S(1)}, u32[]{:S(2)}, u32[]{:S(2)}) collective-permute-start(bf16[1,256,128]{2,1,0:T(8,128)(2,1)S(1)} %collective-permute-done.21), channel_id=1, source_target_pairs={{0,64},{32,96},{64,128},{96,160},{128,192},{160,224},{192,0},{224,... | collective-permute-start | bytes 196616 | tf_op jit(solution)/shard_map/ppermute | solution.py:76
  120.1 6.7 %collective-permute-start.24 = (bf16[1,256,128]{2,1,0:T(8,128)(2,1)S(1)}, bf16[1,256,128]{2,1,0:T(8,128)(2,1)S(1)}, u32[]{:S(2)}, u32[]{:S(2)}) collective-permute-start(bf16[1,256,128]{2,1,0:T(8,128)(2,1)S(1)} %collective-permute-done.22), channel_id=1, source_target_pairs={{0,192},{32,224},{64,0},{96,32},{128,64},{160,96},{192,128},{224,1... | collective-permute-start | bytes 196616 | tf_op jit(solution)/shard_map/ppermute | solution.py:77
  123.5 10.5 %collective-permute-start.15 = (bf16[1,512,128]{2,1,0:T(8,128)(2,1)S(1)}, bf16[1,512,128]{2,1,0:T(8,128)(2,1)S(1)}, u32[]{:S(2)}, u32[]{:S(2)}) collective-permute-start(bf16[1,512,128]{2,1,0:T(8,128)(2,1)S(1)} %get-tuple-element.22), channel_id=1, source_target_pairs={{0,64},{32,96},{64,128},{96,160},{128,192},{160,224},{192,0},{224,... | collective-permute-start | bytes 393224 | tf_op jit(solution)/shard_map/ppermute | solution.py:65
  123.6 10.4 %collective-permute-start.16 = (bf16[1,512,128]{2,1,0:T(8,128)(2,1)S(1)}, bf16[1,512,128]{2,1,0:T(8,128)(2,1)S(1)}, u32[]{:S(2)}, u32[]{:S(2)}) collective-permute-start(bf16[1,512,128]{2,1,0:T(8,128)(2,1)S(1)} %get-tuple-element.23), channel_id=1, source_target_pairs={{0,192},{32,224},{64,0},{96,32},{128,64},{160,96},{192,128},{224,1... | collective-permute-start | bytes 393224 | tf_op jit(solution)/shard_map/ppermute | solution.py:66
  132.4 14.9 %collective-permute-start.27 = (bf16[1,4,512,128]{3,2,1,0:T(8,128)(2,1)S(1)}, bf16[1,4,512,128]{3,2,1,0:T(8,128)(2,1)S(1)}, u32[]{:S(2)}, u32[]{:S(2)}) collective-permute-start(bf16[1,4,512,128]{3,2,1,0:T(8,128)(2,1)S(1)} %bitcast_dynamic-update-slice_fusion.6), channel_id=1, source_target_pairs={{0,32},{32,0},{64,96},{96,64},{128,160},{160,128},{192,224},{224,1... | collective-permute-start | bytes 1572872 | tf_op jit(solution)/shard_map/ppermute | solution.py:80
  134.0 7.0 %collective-permute-start.17 = (bf16[1,512,128]{2,1,0:T(8,128)(2,1)S(1)}, bf16[1,512,128]{2,1,0:T(8,128)(2,1)S(1)}, u32[]{:S(2)}, u32[]{:S(2)}) collective-permute-start(bf16[1,512,128]{2,1,0:T(8,128)(2,1)S(1)} %collective-permute-done.15), channel_id=1, source_target_pairs={{0,64},{32,96},{64,128},{96,160},{128,192},{160,224},{192,0},{224,... | collective-permute-start | bytes 393224 | tf_op jit(solution)/shard_map/ppermute | solution.py:65
  134.0 7.0 %collective-permute-start.18 = (bf16[1,512,128]{2,1,0:T(8,128)(2,1)S(1)}, bf16[1,512,128]{2,1,0:T(8,128)(2,1)S(1)}, u32[]{:S(2)}, u32[]{:S(2)}) collective-permute-start(bf16[1,512,128]{2,1,0:T(8,128)(2,1)S(1)} %collective-permute-done.16), channel_id=1, source_target_pairs={{0,192},{32,224},{64,0},{96,32},{128,64},{160,96},{192,128},{224,1... | collective-permute-start | bytes 393224 | tf_op jit(solution)/shard_map/ppermute | solution.py:66
  141.0 6.2 %collective-permute-start.19 = (bf16[1,512,128]{2,1,0:T(8,128)(2,1)S(1)}, bf16[1,512,128]{2,1,0:T(8,128)(2,1)S(1)}, u32[]{:S(2)}, u32[]{:S(2)}) collective-permute-start(bf16[1,512,128]{2,1,0:T(8,128)(2,1)S(1)} %collective-permute-done.17), channel_id=1, source_target_pairs={{0,64},{32,96},{64,128},{96,160},{128,192},{160,224},{192,0},{224,... | collective-permute-start | bytes 393224 | tf_op jit(solution)/shard_map/ppermute | solution.py:65
  (10 other events, 135.1 us)

commit v4 on v2

--- a/solution.py
+++ b/solution.py
@@ -59,32 +59,32 @@
     relations = grads.shape[1]
     rows = grads.shape[3]
     panel_cols = grads.shape[-1]
-    width = panel_cols * owners
     owned = params.shape[2]
     block = rows // groups
     lead = relations * 2
+    state = jnp.stack([params, moment_one, moment_two]).reshape(3, relations, 2, owned, owners, panel_cols)
+    state = lax.all_to_all(state.transpose(0, 1, 2, 4, 3, 5), "shard", split_axis=3, concat_axis=3, tiled=True)
+    state = state.reshape(3, relations, 2, block, panel_cols)
+    params_p, one_p, two_p = state[0], state[1], state[2]
     local = grads.reshape(lead, groups // 2, 2, block, panel_cols)
-    summed = _reduce_scatter_dp(local, groups)
-    pieces = summed.reshape(relations, 2, owners, owned, panel_cols)
-    moved = lax.all_to_all(pieces, "shard", split_axis=2, concat_axis=2, tiled=True)
-    gradient = moved.transpose(0, 1, 3, 2, 4).reshape(relations, 2, owned, width) / groups
+    gradient = _reduce_scatter_dp(local, groups).reshape(relations, 2, block, panel_cols) / groups
     onehot = (relation_ids[:, None] == jnp.arange(rates.shape[0], dtype=jnp.int32)[None, :]).astype(
         jnp.float32
     )
     learn = jnp.sum(onehot * rates[None, :], axis=1)[:, None, None, None]
-    new_one = 0.9 * moment_one + 0.1 * gradient
-    new_two = 0.95 * moment_two + 0.05 * gradient * gradient
+    new_one = 0.9 * one_p + 0.1 * gradient
+    new_two = 0.95 * two_p + 0.05 * gradient * gradient
     steps = step_count[0].astype(jnp.float32)
     fix_one = 1.0 - jnp.power(jnp.float32(0.9), steps)
     fix_two = 1.0 - jnp.power(jnp.float32(0.95), steps)
-    update = new_one / fix_one / (jnp.sqrt(new_two / fix_two) + 1e-08) + 0.1 * params
-    new_params = params - learn * update
-    fresh = new_params.astype(jnp.bfloat16).reshape(relations, 2, owned, owners, panel_cols)
-    fresh = fresh.transpose(0, 1, 3, 2, 4)
-    back = lax.all_to_all(fresh, "shard", split_axis=2, concat_axis=2, tiled=True)
-    back = back.reshape(lead, block, panel_cols)
-    panels = _all_gather_dp(back, groups).reshape(relations, 2, rows, panel_cols)
-    return (new_params, new_one, new_two, panels)
+    update = new_one / fix_one / (jnp.sqrt(new_two / fix_two) + 1e-08) + 0.1 * params_p
+    new_params = params_p - learn * update
+    fresh = new_params.astype(jnp.bfloat16).reshape(lead, block, panel_cols)
+    panels = _all_gather_dp(fresh, groups).reshape(relations, 2, rows, panel_cols)
+    out = jnp.stack([new_params, new_one, new_two]).reshape(3, relations, 2, owners, owned, panel_cols)
+    out = lax.all_to_all(out, "shard", split_axis=3, concat_axis=3, tiled=True)
+    out = out.transpose(0, 1, 2, 4, 3, 5).reshape(3, relations, 2, owned, owners * panel_cols)
+    return (out[0], out[1], out[2], panels)
 
 
 def solution(mesh):

time: 153 us -> 149 us (0.974)
  blocking collectives: 15.8 us -> 0 us
  local copies, waits for them, and re-layouts: 9.77 us -> 22.6 us
  waiting for transfers between devices: 76.2 us -> 67.7 us
  starting transfers between devices: 36 us -> 43.2 us
    all_to_all x1 -> x0, blocking collectives: 15.8 us -> none  [body(): lax.all_to_all(fresh, 'shard', split_axis=2, concat_axis=2, tiled=True)]
    all_to_all x1 -> x2, waiting for transfers between devices: 15.7 us -> 0.01 us  [the longest x1 0.01 us: body(): out = lax.all_to_all(out, 'shard', split_axis=3, concat_axis=3, tiled=True)]
    all_to_all x1 -> x2, starting transfers between devices: 9.66 us -> 17.6 us  [the longest x1 9.7 us: body(): lax.all_to_all(state.transpose(0, 1, 2, 4, 3, 5), 'shard', split_axis=3,...]
    ppermute x1, waiting for transfers between devices: 6 us -> 12.3 us  [_all_gather_dp(): other = lax.ppermute(mine, 'dp', partner)]
    unnamed x11, local copies, waits for them, and re-layouts: 1.38 us -> 5.77 us
    all_to_all x1, local copies, waits for them, and re-layouts: 0.02 us -> 2.32 us  [body(): out = lax.all_to_all(out, 'shard', split_axis=3, concat_axis=3, tiled=True)]
    ppermute x3, waiting for transfers between devices: 12.3 us -> 14.5 us  [_all_gather_dp(): up = lax.ppermute(up, 'dp', plus)]
    transpose x1, local copies, waits for them, and re-layouts: 0.11 us -> 2.05 us  [body(): state.transpose(0, 1, 2, 4, 3, 5)]
  transfers between devices with their start and end apart: 15 -> 16, of which waited for: 12 -> 11; matrix products, arithmetic and copies ran while one was open for 6% -> 13% of each run, Pallas kernels for 0% -> 0%
where the time goes in v4:
time: 149 us; the launch traced here: 147 us
  waiting for transfers between devices  67.7 us (45%)
  starting transfers between devices  43.2 us (29%)
  local copies, waits for them, and re-layouts  22.6 us (15%)
  other arithmetic  10.9 us (7%)
  between operations  2.24 us (2%)
    ppermute x3, waiting for transfers between devices, _reduce_scatter_dp(): down = lax.ppermute(down, 'dp', minus) + _take(odd, (y + t + 2) % ring)  23.2 us
    ppermute x3, waiting for transfers between devices, _all_gather_dp(): up = lax.ppermute(up, 'dp', plus)  14.5 us
    ppermute x1, waiting for transfers between devices, _all_gather_dp(): other = lax.ppermute(mine, 'dp', partner)  12.3 us
    ppermute x3, starting transfers between devices, _reduce_scatter_dp(): down = lax.ppermute(down, 'dp', minus) + _take(odd, (y + t + 2) % ring)  10.2 us
    ppermute x3, starting transfers between devices, _all_gather_dp(): down = lax.ppermute(down, 'dp', minus)  9.84 us
    all_to_all x1, starting transfers between devices, body(): lax.all_to_all(state.transpose(0, 1, 2, 4, 3, 5), 'shard', split_axis=3,...  9.7 us
    ppermute x3, waiting for transfers between devices, _reduce_scatter_dp(): up = lax.ppermute(up, 'dp', plus) + _take(even, (y - t - 2) % ring)  8.93 us
    ppermute x1, waiting for transfers between devices, _reduce_scatter_dp(): return keep + lax.ppermute(send, 'dp', partner)  8.75 us
  transfers between devices with their start and end apart: 16, of which 11 were waited for; matrix products, arithmetic and copies ran while one was open for 13% of the time, Pallas kernels for 0%

profile of v4, /device:TPU:32, one launch (start us, length us, event | category | flops | bytes accessed | tf_op | source)
XLA Modules:
  0.0 146.6 jit_solution(8481816818467940023)
XLA Ops:
  3.2 2.0 %copy.29 = f32[3,1,2,32,16,128]{5,4,2,1,0,3:T(8,128)} copy(f32[3,1,2,32,16,128]{5,3,0,4,2,1:T(8,128)S(1)} %maximum_bitcast_fusion) | data formatting | bytes 3145728 | tf_op jit(solution)/shard_map/transpose | solution.py:66
  5.3 9.7 %all-to-all-start = ((f32[3,1,2,32,16,128]{5,4,2,1,0,3:T(8,128)}), f32[3,1,2,32,16,128]{5,4,2,1,0,3:T(8,128)}, u32[]{:S(2)}, u32[]{:S(2)}) async-start(f32[3,1,2,32,16,128]{5,4,2,1,0,3:T(8,128)} %copy.29), calls=%async_computation | async-start | bytes 3145728 | tf_op jit(solution)/shard_map/all_to_all | solution.py:66
  15.0 4.0 %fusion.3 = (f32[2,4,1,512,128]{4,3,2,1,0:T(8,128)S(1)}, f32[2,4,1,512,128]{4,3,2,1,0:T(8,128)}) fusion(f32[2,4,2,512,128]{4,3,2,1,0:T(8,128)} %bitcast.99), kind=kLoop, calls=%fused_computation.31 | loop fusion | bytes 8388608 | tf_op jit(solution)/shard_map/slice | solution.py:25
  19.8 3.0 %collective-permute-start.3 = (f32[2,512,128]{2,1,0:T(8,128)}, f32[2,512,128]{2,1,0:T(8,128)S(1)}, u32[]{:S(2)}, u32[]{:S(2)}) collective-permute-start(f32[2,512,128]{2,1,0:T(8,128)} %dynamic-slice_bitcast_fusion), channel_id=1, source_target_pairs={{0,192},{32,224},{64,0},{96,32},{128,64},{160,96},{192,128},{224,1... | collective-permute-start | bytes 1572872 | tf_op jit(solution)/shard_map/ppermute | solution.py:30
  24.7 9.9 %collective-permute-done.3 = f32[2,512,128]{2,1,0:T(8,128)S(1)} collective-permute-done((f32[2,512,128]{2,1,0:T(8,128)}, f32[2,512,128]{2,1,0:T(8,128)S(1)}, u32[]{:S(2)}, u32[]{:S(2)}) %collective-permute-start.3) | collective-permute-done | bytes 524320 | tf_op jit(solution)/shard_map/ppermute | solution.py:30
  35.5 3.6 %collective-permute-start.4 = (f32[2,512,128]{2,1,0:T(8,128)}, f32[2,512,128]{2,1,0:T(8,128)S(1)}, u32[]{:S(2)}, u32[]{:S(2)}) collective-permute-start(f32[2,512,128]{2,1,0:T(8,128)} %bitcast_add_fusion.2), channel_id=1, source_target_pairs={{0,192},{32,224},{64,0},{96,32},{128,64},{160,96},{192,128},{224,1... | collective-permute-start | bytes 1572872 | tf_op jit(solution)/shard_map/ppermute | solution.py:30
  41.7 8.4 %collective-permute-done.4 = f32[2,512,128]{2,1,0:T(8,128)S(1)} collective-permute-done((f32[2,512,128]{2,1,0:T(8,128)}, f32[2,512,128]{2,1,0:T(8,128)S(1)}, u32[]{:S(2)}, u32[]{:S(2)}) %collective-permute-start.4) | collective-permute-done | bytes 524320 | tf_op jit(solution)/shard_map/ppermute | solution.py:30
  50.9 3.6 %collective-permute-start.5 = (f32[2,512,128]{2,1,0:T(8,128)}, f32[2,512,128]{2,1,0:T(8,128)S(1)}, u32[]{:S(2)}, u32[]{:S(2)}) collective-permute-start(f32[2,512,128]{2,1,0:T(8,128)} %bitcast_add_fusion.1), channel_id=1, source_target_pairs={{0,192},{32,224},{64,0},{96,32},{128,64},{160,96},{192,128},{224,1... | collective-permute-start | bytes 1572872 | tf_op jit(solution)/shard_map/ppermute | solution.py:30
  59.9 4.9 %collective-permute-done.5 = f32[2,512,128]{2,1,0:T(8,128)S(1)} collective-permute-done((f32[2,512,128]{2,1,0:T(8,128)}, f32[2,512,128]{2,1,0:T(8,128)S(1)}, u32[]{:S(2)}, u32[]{:S(2)}) %collective-permute-start.5) | collective-permute-done | bytes 524320 | tf_op jit(solution)/shard_map/ppermute | solution.py:30
  64.8 6.7 %collective-permute-done.2 = f32[2,512,128]{2,1,0:T(8,128)S(1)} collective-permute-done((f32[2,512,128]{2,1,0:T(8,128)}, f32[2,512,128]{2,1,0:T(8,128)S(1)}, u32[]{:S(2)}, u32[]{:S(2)}) %collective-permute-start.2) | collective-permute-done | bytes 524320 | tf_op jit(solution)/shard_map/ppermute | solution.py:29
  71.5 1.9 %broadcast_select_fusion.2 = f32[2,512,128]{2,1,0:T(8,128)} fusion(pred[]{:T(512)S(6)} %eq.37, f32[2,512,128]{2,1,0:T(8,128)S(1)} %collective-permute-done.2, f32[2,4,1,512,128]{4,3,2,1,0:T(8,128)} %get-tuple-element.13, s32[]{:T(128)S(6)} %select_n.120, f32[2,512,128]{2,1,0:T(8,128)S(1)} %collective-permute-done.5, ...), kind=kLoop, calls=%fused_computation.27 | loop fusion | flops 393216 | bytes 2621449 | tf_op jit(solution)/shard_map/select_n | solution.py:32
  73.4 2.7 %collective-permute-start.6 = (f32[2,512,128]{2,1,0:T(8,128)}, f32[2,512,128]{2,1,0:T(8,128)}, u32[]{:S(2)}, u32[]{:S(2)}) collective-permute-start(f32[2,512,128]{2,1,0:T(8,128)} %broadcast_select_fusion.2), channel_id=1, source_target_pairs={{0,32},{32,0},{64,96},{96,64},{128,160},{160,128},{192,224},{224,1... | collective-permute-start | bytes 1572872 | tf_op jit(solution)/shard_map/ppermute | solution.py:33
  77.8 8.8 %collective-permute-done.6 = f32[2,512,128]{2,1,0:T(8,128)} collective-permute-done((f32[2,512,128]{2,1,0:T(8,128)}, f32[2,512,128]{2,1,0:T(8,128)}, u32[]{:S(2)}, u32[]{:S(2)}) %collective-permute-start.6) | collective-permute-done | bytes 524320 | tf_op jit(solution)/shard_map/ppermute | solution.py:33
  86.5 2.3 %fusion.2 = (bf16[2,512,128]{2,1,0:T(8,128)(2,1)S(1)}, f32[2,512,128]{2,1,0:T(8,128)S(1)}, f32[2,512,128]{2,1,0:T(8,128)S(1)}, f32[2,512,128]{2,1,0:T(8,128)S(1)}) fusion(f32[2,512,128]{2,1,0:T(8,128)S(1)} %bitcast.100, f32[]{:T(128)} %bitcast.15, f32[]{:T(128)} %bitcast.13, f32[]{:T(128)} %fusion.1, f32[2,512,128]{2,1,0:T(8,128)S(1)} %bitcast.102, ...), kind=kLoop, calls=%fused_computation.30 | loop fusion | flops 2490368 | bytes 6029333 | tf_op jit(solution)/shard_map/convert_element_type | solution.py:82
  90.4 7.9 %all-to-all-start.1 = ((f32[3,1,2,32,16,128]{5,4,2,1,0,3:T(8,128)}), f32[3,1,2,32,16,128]{5,4,2,1,0,3:T(8,128)}, u32[]{:S(2)}, u32[]{:S(2)}) async-start(f32[3,1,2,32,16,128]{5,4,2,1,0,3:T(8,128)} %copy.35), calls=%async_computation.1 | async-start | bytes 3145728 | tf_op jit(solution)/shard_map/all_to_all | solution.py:85
  98.3 2.8 %collective-permute-start.7 = (bf16[2,512,128]{2,1,0:T(8,128)(2,1)S(1)}, bf16[2,512,128]{2,1,0:T(8,128)(2,1)S(1)}, u32[]{:S(2)}, u32[]{:S(2)}) collective-permute-start(bf16[2,512,128]{2,1,0:T(8,128)(2,1)S(1)} %get-tuple-element.8), channel_id=1, source_target_pairs={{0,32},{32,0},{64,96},{96,64},{128,160},{160,128},{192,224},{224,1... | collective-permute-start | bytes 786440 | tf_op jit(solution)/shard_map/ppermute | solution.py:41
  101.1 12.3 %collective-permute-done.7 = bf16[2,512,128]{2,1,0:T(8,128)(2,1)S(1)} collective-permute-done((bf16[2,512,128]{2,1,0:T(8,128)(2,1)S(1)}, bf16[2,512,128]{2,1,0:T(8,128)(2,1)S(1)}, u32[]{:S(2)}, u32[]{:S(2)}) %collective-permute-start.7) | collective-permute-done | bytes 262176 | tf_op jit(solution)/shard_map/ppermute | solution.py:41
  113.6 3.2 %collective-permute-start.9 = (bf16[2,512,128]{2,1,0:T(8,128)(2,1)S(1)}, bf16[2,512,128]{2,1,0:T(8,128)(2,1)S(1)}, u32[]{:S(2)}, u32[]{:S(2)}) collective-permute-start(bf16[2,512,128]{2,1,0:T(8,128)(2,1)S(1)} %get-tuple-element.21), channel_id=1, source_target_pairs={{0,192},{32,224},{64,0},{96,32},{128,64},{160,96},{192,128},{224,1... | collective-permute-start | bytes 786440 | tf_op jit(solution)/shard_map/ppermute | solution.py:50
  117.3 5.3 %collective-permute-done.8 = bf16[2,512,128]{2,1,0:T(8,128)(2,1)S(1)} collective-permute-done((bf16[2,512,128]{2,1,0:T(8,128)(2,1)S(1)}, bf16[2,512,128]{2,1,0:T(8,128)(2,1)S(1)}, u32[]{:S(2)}, u32[]{:S(2)}) %collective-permute-start.8) | collective-permute-done | bytes 262176 | tf_op jit(solution)/shard_map/ppermute | solution.py:49
  122.7 3.3 %collective-permute-start.11 = (bf16[2,512,128]{2,1,0:T(8,128)(2,1)S(1)}, bf16[2,512,128]{2,1,0:T(8,128)(2,1)S(1)}, u32[]{:S(2)}, u32[]{:S(2)}) collective-permute-start(bf16[2,512,128]{2,1,0:T(8,128)(2,1)S(1)} %collective-permute-done.9), channel_id=1, source_target_pairs={{0,192},{32,224},{64,0},{96,32},{128,64},{160,96},{192,128},{224,1... | collective-permute-start | bytes 786440 | tf_op jit(solution)/shard_map/ppermute | solution.py:50
  126.1 4.9 %collective-permute-done.10 = bf16[2,512,128]{2,1,0:T(8,128)(2,1)S(1)} collective-permute-done((bf16[2,512,128]{2,1,0:T(8,128)(2,1)S(1)}, bf16[2,512,128]{2,1,0:T(8,128)(2,1)S(1)}, u32[]{:S(2)}, u32[]{:S(2)}) %collective-permute-start.10) | collective-permute-done | bytes 262176 | tf_op jit(solution)/shard_map/ppermute | solution.py:49
  131.0 3.3 %collective-permute-start.13 = (bf16[2,512,128]{2,1,0:T(8,128)(2,1)S(1)}, bf16[2,512,128]{2,1,0:T(8,128)(2,1)S(1)}, u32[]{:S(2)}, u32[]{:S(2)}) collective-permute-start(bf16[2,512,128]{2,1,0:T(8,128)(2,1)S(1)} %collective-permute-done.11), channel_id=1, source_target_pairs={{0,192},{32,224},{64,0},{96,32},{128,64},{160,96},{192,128},{224,1... | collective-permute-start | bytes 786440 | tf_op jit(solution)/shard_map/ppermute | solution.py:50
  134.4 4.2 %collective-permute-done.12 = bf16[2,512,128]{2,1,0:T(8,128)(2,1)S(1)} collective-permute-done((bf16[2,512,128]{2,1,0:T(8,128)(2,1)S(1)}, bf16[2,512,128]{2,1,0:T(8,128)(2,1)S(1)}, u32[]{:S(2)}, u32[]{:S(2)}) %collective-permute-start.12) | collective-permute-done | bytes 262176 | tf_op jit(solution)/shard_map/ppermute | solution.py:49
  140.9 2.3 %copy.61 = f32[3,1,2,32,16,128]{5,3,0,4,2,1:T(8,128)S(1)} copy(f32[3,1,2,32,16,128]{5,4,2,1,0,3:T(8,128)} %all-to-all-done.1) | data formatting | bytes 3145728 | tf_op jit(solution)/shard_map/all_to_all | solution.py:85
  (47 shorter events, 23.3 us)
Async XLA Ops:
  0.6 2.3 %copy-start = (f32[1,2,16,4096]{3,2,1,0:T(8,128)S(1)}, f32[1,2,16,4096]{3,2,1,0:T(8,128)}, u32[]{:S(2)}) copy-start(f32[1,2,16,4096]{3,2,1,0:T(8,128)} %param.10) | copy-start | bytes 1572868
  5.3 70.9 %all-to-all-start = ((f32[3,1,2,32,16,128]{5,4,2,1,0,3:T(8,128)}), f32[3,1,2,32,16,128]{5,4,2,1,0,3:T(8,128)}, u32[]{:S(2)}, u32[]{:S(2)}) async-start(f32[3,1,2,32,16,128]{5,4,2,1,0,3:T(8,128)} %copy.29), calls=%async_computation | async-start | bytes 3145728 | tf_op jit(solution)/shard_map/all_to_all | solution.py:66
  19.8 14.8 %collective-permute-start.3 = (f32[2,512,128]{2,1,0:T(8,128)}, f32[2,512,128]{2,1,0:T(8,128)S(1)}, u32[]{:S(2)}, u32[]{:S(2)}) collective-permute-start(f32[2,512,128]{2,1,0:T(8,128)} %dynamic-slice_bitcast_fusion), channel_id=1, source_target_pairs={{0,192},{32,224},{64,0},{96,32},{128,64},{160,96},{192,128},{224,1... | collective-permute-start | bytes 1572872 | tf_op jit(solution)/shard_map/ppermute | solution.py:30
  24.7 15.1 %collective-permute-start = (f32[2,512,128]{2,1,0:T(8,128)}, f32[2,512,128]{2,1,0:T(8,128)S(1)}, u32[]{:S(2)}, u32[]{:S(2)}) collective-permute-start(f32[2,512,128]{2,1,0:T(8,128)} %dynamic-slice_bitcast_fusion.1), channel_id=1, source_target_pairs={{0,64},{32,96},{64,128},{96,160},{128,192},{160,224},{192,0},{224,... | collective-permute-start | bytes 1572872 | tf_op jit(solution)/shard_map/ppermute | solution.py:29
  35.5 23.8 %copy-start.1 = (f32[64]{0:T(128)S(1)}, f32[64]{0:T(128)}, u32[]{:S(2)}) copy-start(f32[64]{0:T(128)} %param.12) | copy-start | bytes 772
  35.5 14.6 %collective-permute-start.4 = (f32[2,512,128]{2,1,0:T(8,128)}, f32[2,512,128]{2,1,0:T(8,128)S(1)}, u32[]{:S(2)}, u32[]{:S(2)}) collective-permute-start(f32[2,512,128]{2,1,0:T(8,128)} %bitcast_add_fusion.2), channel_id=1, source_target_pairs={{0,192},{32,224},{64,0},{96,32},{128,64},{160,96},{192,128},{224,1... | collective-permute-start | bytes 1572872 | tf_op jit(solution)/shard_map/ppermute | solution.py:30
  41.7 14.3 %collective-permute-start.1 = (f32[2,512,128]{2,1,0:T(8,128)}, f32[2,512,128]{2,1,0:T(8,128)S(1)}, u32[]{:S(2)}, u32[]{:S(2)}) collective-permute-start(f32[2,512,128]{2,1,0:T(8,128)} %bitcast_add_fusion.5), channel_id=1, source_target_pairs={{0,64},{32,96},{64,128},{96,160},{128,192},{160,224},{192,0},{224,... | collective-permute-start | bytes 1572872 | tf_op jit(solution)/shard_map/ppermute | solution.py:29
  50.9 13.9 %collective-permute-start.5 = (f32[2,512,128]{2,1,0:T(8,128)}, f32[2,512,128]{2,1,0:T(8,128)S(1)}, u32[]{:S(2)}, u32[]{:S(2)}) collective-permute-start(f32[2,512,128]{2,1,0:T(8,128)} %bitcast_add_fusion.1), channel_id=1, source_target_pairs={{0,192},{32,224},{64,0},{96,32},{128,64},{160,96},{192,128},{224,1... | collective-permute-start | bytes 1572872 | tf_op jit(solution)/shard_map/ppermute | solution.py:30
  57.9 13.6 %collective-permute-start.2 = (f32[2,512,128]{2,1,0:T(8,128)}, f32[2,512,128]{2,1,0:T(8,128)S(1)}, u32[]{:S(2)}, u32[]{:S(2)}) collective-permute-start(f32[2,512,128]{2,1,0:T(8,128)} %bitcast_add_fusion.4), channel_id=1, source_target_pairs={{0,64},{32,96},{64,128},{96,160},{128,192},{160,224},{192,0},{224,... | collective-permute-start | bytes 1572872 | tf_op jit(solution)/shard_map/ppermute | solution.py:29
  73.4 13.1 %collective-permute-start.6 = (f32[2,512,128]{2,1,0:T(8,128)}, f32[2,512,128]{2,1,0:T(8,128)}, u32[]{:S(2)}, u32[]{:S(2)}) collective-permute-start(f32[2,512,128]{2,1,0:T(8,128)} %broadcast_select_fusion.2), channel_id=1, source_target_pairs={{0,32},{32,0},{64,96},{96,64},{128,160},{160,128},{192,224},{224,1... | collective-permute-start | bytes 1572872 | tf_op jit(solution)/shard_map/ppermute | solution.py:33
  90.4 50.4 %all-to-all-start.1 = ((f32[3,1,2,32,16,128]{5,4,2,1,0,3:T(8,128)}), f32[3,1,2,32,16,128]{5,4,2,1,0,3:T(8,128)}, u32[]{:S(2)}, u32[]{:S(2)}) async-start(f32[3,1,2,32,16,128]{5,4,2,1,0,3:T(8,128)} %copy.35), calls=%async_computation.1 | async-start | bytes 3145728 | tf_op jit(solution)/shard_map/all_to_all | solution.py:85
  98.3 15.2 %collective-permute-start.7 = (bf16[2,512,128]{2,1,0:T(8,128)(2,1)S(1)}, bf16[2,512,128]{2,1,0:T(8,128)(2,1)S(1)}, u32[]{:S(2)}, u32[]{:S(2)}) collective-permute-start(bf16[2,512,128]{2,1,0:T(8,128)(2,1)S(1)} %get-tuple-element.8), channel_id=1, source_target_pairs={{0,32},{32,0},{64,96},{96,64},{128,160},{160,128},{192,224},{224,1... | collective-permute-start | bytes 786440 | tf_op jit(solution)/shard_map/ppermute | solution.py:41
  113.5 9.2 %collective-permute-start.8 = (bf16[2,512,128]{2,1,0:T(8,128)(2,1)S(1)}, bf16[2,512,128]{2,1,0:T(8,128)(2,1)S(1)}, u32[]{:S(2)}, u32[]{:S(2)}) collective-permute-start(bf16[2,512,128]{2,1,0:T(8,128)(2,1)S(1)} %get-tuple-element.20), channel_id=1, source_target_pairs={{0,64},{32,96},{64,128},{96,160},{128,192},{160,224},{192,0},{224,... | collective-permute-start | bytes 786440 | tf_op jit(solution)/shard_map/ppermute | solution.py:49
  113.6 9.1 %collective-permute-start.9 = (bf16[2,512,128]{2,1,0:T(8,128)(2,1)S(1)}, bf16[2,512,128]{2,1,0:T(8,128)(2,1)S(1)}, u32[]{:S(2)}, u32[]{:S(2)}) collective-permute-start(bf16[2,512,128]{2,1,0:T(8,128)(2,1)S(1)} %get-tuple-element.21), channel_id=1, source_target_pairs={{0,192},{32,224},{64,0},{96,32},{128,64},{160,96},{192,128},{224,1... | collective-permute-start | bytes 786440 | tf_op jit(solution)/shard_map/ppermute | solution.py:50
  122.7 8.3 %collective-permute-start.10 = (bf16[2,512,128]{2,1,0:T(8,128)(2,1)S(1)}, bf16[2,512,128]{2,1,0:T(8,128)(2,1)S(1)}, u32[]{:S(2)}, u32[]{:S(2)}) collective-permute-start(bf16[2,512,128]{2,1,0:T(8,128)(2,1)S(1)} %collective-permute-done.8), channel_id=1, source_target_pairs={{0,64},{32,96},{64,128},{96,160},{128,192},{160,224},{192,0},{224,... | collective-permute-start | bytes 786440 | tf_op jit(solution)/shard_map/ppermute | solution.py:49
  122.7 8.3 %collective-permute-start.11 = (bf16[2,512,128]{2,1,0:T(8,128)(2,1)S(1)}, bf16[2,512,128]{2,1,0:T(8,128)(2,1)S(1)}, u32[]{:S(2)}, u32[]{:S(2)}) collective-permute-start(bf16[2,512,128]{2,1,0:T(8,128)(2,1)S(1)} %collective-permute-done.9), channel_id=1, source_target_pairs={{0,192},{32,224},{64,0},{96,32},{128,64},{160,96},{192,128},{224,1... | collective-permute-start | bytes 786440 | tf_op jit(solution)/shard_map/ppermute | solution.py:50
  131.0 7.6 %collective-permute-start.12 = (bf16[2,512,128]{2,1,0:T(8,128)(2,1)S(1)}, bf16[2,512,128]{2,1,0:T(8,128)(2,1)S(1)}, u32[]{:S(2)}, u32[]{:S(2)}) collective-permute-start(bf16[2,512,128]{2,1,0:T(8,128)(2,1)S(1)} %collective-permute-done.10), channel_id=1, source_target_pairs={{0,64},{32,96},{64,128},{96,160},{128,192},{160,224},{192,0},{224,... | collective-permute-start | bytes 786440 | tf_op jit(solution)/shard_map/ppermute | solution.py:49
  131.0 9.1 %collective-permute-start.13 = (bf16[2,512,128]{2,1,0:T(8,128)(2,1)S(1)}, bf16[2,512,128]{2,1,0:T(8,128)(2,1)S(1)}, u32[]{:S(2)}, u32[]{:S(2)}) collective-permute-start(bf16[2,512,128]{2,1,0:T(8,128)(2,1)S(1)} %collective-permute-done.11), channel_id=1, source_target_pairs={{0,192},{32,224},{64,0},{96,32},{128,64},{160,96},{192,128},{224,1... | collective-permute-start | bytes 786440 | tf_op jit(solution)/shard_map/ppermute | solution.py:50
